TPU v7x, 128 devices: a whole 4x4x4 slice. The times are simulated.
128 devices in a mesh: ctx: 16 (over x, y_hi, core), head: 8 (over z, y_lo).
Axes of the slice: x: 4, y: 4 (y_hi: 2, y_lo: 2; y = y_hi * 2 + y_lo), z: 4, core: 2. Of those that a mesh axis runs over, the one named last changes fastest.
Arguments:
- activations: bfloat16 [8192, 4096], P('ctx')
- qkv_weight: bfloat16 [4096, 3, 32, 128], P(None, None, 'head'), may hold values from -0.09375 to 0.09375
- out_weight: bfloat16 [32, 128, 4096], P('head'), may hold values from -0.09375 to 0.09375
- mod_table: float32 [16, 4096], replicated, may hold values from -3 to 3
- clip_level: int32 [64], replicated, may hold values from 0 to 15
- clip_of: int32 [8192], P('ctx'), may hold values from 0 to 63, never falling along the last dimension, each value on 1 to 256 neighbouring positions
- visible: int32 [64, 64], replicated, may hold values from 0 to 1, as said below
Outputs:
- mixed: bfloat16 [8192, 4096], P(('ctx', 'head'))
Inputs may be any that keep to these rules, and one draw needn't show every extreme that they name: visible is 1 on the diagonal and 0 above it. `clip_of`: clip numbers never fall along the tokens; every clip has 1 to 256 tokens and one has exactly 256.
All inputs are finite; a program needn't handle non-finite values.
Results may differ from a plain program's by a relative error of at most 0.02.
The roundings to bfloat16 on the way count: a program that leaves them out, or rounds other values in their place, can miss the bound.
Values may be sent and summed in bfloat16 or wider, within the bound.
No kernel may reach another device: no remote copies, remote signals or barrier semaphores. Data moves between devices by JAX's collectives and lax.ppermute only.
A program may use at most 128 MiB of HBM per device.

v0:
```python
import functools
import math

import jax
import numpy as np
import jax.numpy as jnp
from jax import lax
from jax.experimental import pallas as pl
from jax.experimental.pallas import tpu as pltpu
from jax.sharding import Mesh, PartitionSpec as P


def attn_body(qvis_ref, q_ref, k_ref, v_ref, kh_ref, m_sc, l_sc, acc_sc, scale):
    lanes = m_sc.shape[1]
    allowed = jnp.dot(qvis_ref[...], kh_ref[...], preferred_element_type=jnp.float32)
    s = lax.dot_general(q_ref[...], k_ref[...], (((1,), (1,)), ((), ())), preferred_element_type=jnp.float32)
    bk = s.shape[1]
    s = jnp.where(allowed > 0.5, s * scale, -jnp.inf)
    m_old = m_sc[...]
    m_new = jnp.maximum(m_old, jnp.max(s, axis=1, keepdims=True))
    p = jnp.exp2(s - jnp.tile(m_new, (1, bk // lanes)))
    alpha = jnp.exp2(m_old - m_new)
    l_sc[...] = l_sc[...] * alpha + jnp.sum(p, axis=1, keepdims=True)
    acc_sc[...] = acc_sc[...] * alpha + jnp.dot(
        p.astype(jnp.bfloat16), v_ref[...], preferred_element_type=jnp.float32
    )
    m_sc[...] = m_new


def local_kernel(qvis_ref, q_ref, k_ref, v_ref, kh_ref, m_ref, l_ref, acc_ref, *, scale):
    j = pl.program_id(0)

    @pl.when(j == 0)
    def _():
        m_ref[...] = jnp.full(m_ref.shape, -1e30, jnp.float32)
        l_ref[...] = jnp.zeros(l_ref.shape, jnp.float32)
        acc_ref[...] = jnp.zeros(acc_ref.shape, jnp.float32)

    attn_body(qvis_ref, q_ref, k_ref, v_ref, kh_ref, m_ref, l_ref, acc_ref, scale)


def remote_kernel(own_ref, qvis_ref, q_ref, k_ref, v_ref, kh_ref, m_in, l_in, acc_in, o_ref, m_sc, l_sc, acc_sc, *, scale, nsteps):
    j = pl.program_id(0)

    @pl.when(j == 0)
    def _():
        m_sc[...] = m_in[...]
        l_sc[...] = l_in[...]
        acc_sc[...] = acc_in[...]

    attn_body(qvis_ref, q_ref, k_ref, v_ref, kh_ref, m_sc, l_sc, acc_sc, scale)

    @pl.when(j == nsteps - 1)
    def _():
        o_ref[...] = (acc_sc[...] / l_sc[...]).astype(o_ref.dtype)


def carry_kernel(own_ref, qvis_ref, q_ref, k_ref, v_ref, kh_ref, m_in, l_in, acc_in, m_ref, l_ref, acc_ref, *, scale):
    j = pl.program_id(0)

    @pl.when(j == 0)
    def _():
        m_ref[...] = m_in[...]
        l_ref[...] = l_in[...]
        acc_ref[...] = acc_in[...]

    attn_body(qvis_ref, q_ref, k_ref, v_ref, kh_ref, m_ref, l_ref, acc_ref, scale)


def attend_local(qvis, q, keys, values, key_hot, scale):
    nq, hd = q.shape
    tok = keys.shape[0]
    clip_count = qvis.shape[1]
    bk = math.gcd(tok, 1024)
    nsteps = tok // bk
    state = jax.ShapeDtypeStruct((nq, 128), jnp.float32)
    return pl.pallas_call(
        functools.partial(local_kernel, scale=scale),
        grid=(nsteps,),
        in_specs=[
            pl.BlockSpec((nq, clip_count), lambda j: (0, 0)),
            pl.BlockSpec((nq, hd), lambda j: (0, 0)),
            pl.BlockSpec((bk, hd), lambda j: (j, 0)),
            pl.BlockSpec((bk, hd), lambda j: (j, 0)),
            pl.BlockSpec((clip_count, bk), lambda j: (0, j)),
        ],
        out_specs=[
            pl.BlockSpec((nq, 128), lambda j: (0, 0)),
            pl.BlockSpec((nq, 128), lambda j: (0, 0)),
            pl.BlockSpec((nq, hd), lambda j: (0, 0)),
        ],
        out_shape=[state, state, jax.ShapeDtypeStruct((nq, hd), jnp.float32)],
        compiler_params=pltpu.CompilerParams(dimension_semantics=("arbitrary",)),
        cost_estimate=pl.CostEstimate(
            flops=4 * nq * tok * hd + 2 * nq * clip_count * tok,
            transcendentals=nq * tok,
            bytes_accessed=4 * tok * hd + 3 * nq * 512,
        ),
    )(qvis, q, keys, values, key_hot)


def attend_remote(own, qvis, q, kv_all, key_hot, carry, scale, tok, finalize):
    nq, hd = q.shape
    sources = kv_all.shape[0]
    clip_count = qvis.shape[1]
    bk = math.gcd(tok, 1024)
    sub = tok // bk
    nsteps = (sources - 1) * sub

    def src(j, o):
        return (o[0] + 1 + j // sub) % sources

    state_specs = [
        pl.BlockSpec((nq, 128), lambda j, o: (0, 0)),
        pl.BlockSpec((nq, 128), lambda j, o: (0, 0)),
        pl.BlockSpec((nq, hd), lambda j, o: (0, 0)),
    ]
    if finalize:
        kernel = functools.partial(remote_kernel, scale=scale, nsteps=nsteps)
        out_specs = pl.BlockSpec((nq, hd), lambda j, o: (0, 0))
        out_shape = jax.ShapeDtypeStruct((nq, hd), jnp.bfloat16)
        scratch = [
            pltpu.VMEM((nq, 128), jnp.float32),
            pltpu.VMEM((nq, 128), jnp.float32),
            pltpu.VMEM((nq, hd), jnp.float32),
        ]
    else:
        kernel = functools.partial(carry_kernel, scale=scale)
        out_specs = state_specs
        state = jax.ShapeDtypeStruct((nq, 128), jnp.float32)
        out_shape = [state, state, jax.ShapeDtypeStruct((nq, hd), jnp.float32)]
        scratch = []
    grid_spec = pltpu.PrefetchScalarGridSpec(
        num_scalar_prefetch=1,
        grid=(nsteps,),
        in_specs=[
            pl.BlockSpec((nq, clip_count), lambda j, o: (0, 0)),
            pl.BlockSpec((nq, hd), lambda j, o: (0, 0)),
            pl.BlockSpec((None, bk, hd), lambda j, o: (src(j, o), j % sub, 0)),
            pl.BlockSpec((None, bk, hd), lambda j, o: (src(j, o), sub + j % sub, 0)),
            pl.BlockSpec((None, clip_count, bk), lambda j, o: (src(j, o), 0, j % sub)),
        ] + state_specs,
        out_specs=out_specs,
        scratch_shapes=scratch,
    )
    return pl.pallas_call(
        kernel,
        grid_spec=grid_spec,
        out_shape=out_shape,
        compiler_params=pltpu.CompilerParams(dimension_semantics=("arbitrary",)),
        cost_estimate=pl.CostEstimate(
            flops=4 * nq * (sources - 1) * tok * hd + 2 * nq * clip_count * (sources - 1) * tok,
            transcendentals=nq * (sources - 1) * tok,
            bytes_accessed=kv_all.size * 2 + 3 * nq * 512,
        ),
    )(own, qvis, q, kv_all, kv_all, key_hot, *carry)


def per_device_body(activations, qkv_weight, out_weight, mod_table, clip_level, clip_of, visible):
    heads_here = qkv_weight.shape[2]
    head_size = qkv_weight.shape[3]
    clip_count = visible.shape[0]
    level_count = mod_table.shape[0]
    tok = clip_of.shape[0]
    clip_ids = lax.broadcasted_iota(jnp.int32, (1, clip_count), 1)
    level_ids = lax.broadcasted_iota(jnp.int32, (1, level_count), 1)
    tok_hot = clip_of[:, None] == clip_ids
    level_rows = jnp.sum(jnp.where(tok_hot, clip_level[None, :], 0), axis=1)
    level_hot = (level_rows[:, None] == level_ids).astype(jnp.float32)
    modulation = jnp.dot(level_hot, mod_table, precision=lax.Precision.HIGHEST)
    moduled = (activations.astype(jnp.float32) * (1.0 + modulation)).astype(jnp.bfloat16)
    qkv = jnp.einsum(
        "td,dchk->hctk", moduled, qkv_weight, preferred_element_type=jnp.float32
    ).astype(jnp.bfloat16)
    lane = head_size
    clip_rows = tok // lane
    pad_rows = -clip_rows % 8
    clip_slab = jnp.concatenate(
        [clip_of.astype(jnp.bfloat16).reshape(clip_rows, lane), jnp.zeros((pad_rows, lane), jnp.bfloat16)]
    )
    payload = jnp.concatenate(
        [qkv.reshape(heads_here, 3 * tok, lane), jnp.broadcast_to(clip_slab, (heads_here,) + clip_slab.shape)],
        axis=1,
    )
    exch = lax.all_to_all(payload, "yc", 0, 0, tiled=True)
    group_tok = heads_here * tok
    queries = exch[:, 0:tok].reshape(group_tok, lane)
    keys = exch[:, tok:2 * tok].reshape(group_tok, lane)
    values = exch[:, 2 * tok:3 * tok].reshape(group_tok, lane)
    clip_group = exch[:, 3 * tok:3 * tok + clip_rows].reshape(group_tok)
    halves = 2
    half_tok = group_tok // halves
    half_rows = half_tok // lane
    kv_pad = -half_rows % 8
    payloads = [
        jnp.concatenate(
            [
                keys[i * half_tok:(i + 1) * half_tok],
                values[i * half_tok:(i + 1) * half_tok],
                clip_group[i * half_tok:(i + 1) * half_tok].reshape(half_rows, lane),
                jnp.zeros((kv_pad, lane), jnp.bfloat16),
            ]
        )
        for i in range(halves)
    ]
    query_hot = (clip_group.astype(jnp.int32)[:, None] == clip_ids).astype(jnp.float32)
    qvis = jnp.dot(query_hot, visible.astype(jnp.float32), precision=lax.Precision.HIGHEST).astype(jnp.bfloat16)
    score_scale = float(np.float32(1.0) / np.sqrt(np.float32(head_size)) * np.float32(math.log2(math.e)))
    local_hot = (clip_group.astype(jnp.int32)[None, :] == clip_ids[0][:, None]).astype(jnp.bfloat16)
    carry = attend_local(qvis, queries, keys, values, local_hot, score_scale)
    own = lax.axis_index("x").reshape(1).astype(jnp.int32)
    gathered = []
    for i in range(halves):
        gathered.append(lax.all_gather(payloads[i], "x", axis=0))
    for i in range(halves):
        kv_all = gathered[i]
        key_clips = kv_all[:, 2 * half_tok:2 * half_tok + half_rows].reshape(kv_all.shape[0], half_tok)
        key_hot = (key_clips.astype(jnp.int32)[:, None, :] == clip_ids[0][None, :, None]).astype(jnp.bfloat16)
        carry = attend_remote(own, qvis, queries, kv_all, key_hot, carry, score_scale, half_tok, i == halves - 1)
    attended = carry
    back = lax.all_to_all(attended.reshape(heads_here, tok, lane), "yc", 0, 0, tiled=True)
    mixed = jnp.einsum(
        "hrd,hdo->ro", back, out_weight, preferred_element_type=jnp.float32
    ).astype(jnp.bfloat16)
    groups = lax.axis_size("head")
    parts = mixed.reshape(groups, mixed.shape[0] // groups, mixed.shape[1])
    parts = lax.all_to_all(parts, "head", 0, 0)
    return jnp.sum(parts.astype(jnp.float32), axis=0).astype(jnp.bfloat16)


def solution(mesh):
    ctx = mesh.shape["ctx"]
    heads = 4
    fine = Mesh(mesh.devices.reshape(ctx // heads, heads, mesh.shape["head"]), ("x", "yc", "head"))
    placed = (
        P(("x", "yc"), None),
        P(None, None, "head", None),
        P("head", None, None),
        P(),
        P(),
        P(("x", "yc")),
        P(),
    )
    return jax.shard_map(
        per_device_body, mesh=fine, in_specs=placed, out_specs=P(("x", "yc", "head"), None), check_vma=False
    )
```

profile of v0, /device:TPU:6, one launch (start us, length us, event | category | flops | bytes accessed | tf_op | source)
XLA Modules:
  0.0 231.9 jit_solution(13658289422906948866)
XLA Ops:
  6.5 0.7 convert_bitcast_fusion.2
  7.3 0.8 select_reduce_fusion
  8.1 5.6 %fusion.2 = bf16[512,4096,1,1]{1,0,3,2:T(8,128)(2,1)S(1)} fusion(f32[16,4096]{1,0:T(8,128)S(1)} %copy-done, bf16[512,4096]{1,0:T(8,128)(2,1)} %param.7, s32[512]{0:T(512)S(1)} %select_reduce_fusion), kind=kOutput, calls=%fused_computation.4 | convolution fusion | flops 411049984 | bytes 8652800 | tf_op jit(solution)/shard_map/dot_general | solution.py:170
  13.7 10.0 %fusion.6 = bf16[4,3,512,128]{3,2,0,1:T(8,128)(2,1)S(1)} fusion(bf16[512,4096,1,1]{1,0,3,2:T(8,128)(2,1)S(1)} %fusion.2, bf16[4096,3,4,128]{3,2,1,0:T(4,128)(2,1)} %param.8), kind=kOutput, calls=%fused_computation.8 | convolution fusion | flops 6443237376 | bytes 18350080 | tf_op jit(solution)/shard_map/td,dchk->hctk/dot_general | solution.py:172
  24.0 25.9 %all_to_all.15 = bf16[4,1544,128]{2,1,0:T(8,128)(2,1)S(1)} all-to-all(bf16[4,1544,128]{2,1,0:T(8,128)(2,1)S(1)} %pad_maximum_fusion), channel_id=1, replica_groups=mesh['x'=4,'yc'=4,'head'=8] {'yc'}, dimensions={0} | all-to-all | bytes 3162112 | tf_op jit(solution)/shard_map/all_to_all | solution.py:185
  50.0 0.9 pad_maximum_fusion.2
  50.9 0.2 all-gather.5.cloned.1.call-start
  51.1 0.8 pad_maximum_fusion.1
  52.0 1.5 convolution_convert_fusion.qvis_ref
  53.5 1.3 fusion.15
  54.8 0.7 fusion.12.kh_ref
  55.5 11.6 %shard_map.73 = (f32[2048,128]{1,0:T(8,128)}, f32[2048,128]{1,0:T(8,128)}, f32[2048,128]{1,0:T(8,128)}) custom-call(bf16[2048,64]{1,0:T(8,128)(2,1)} %convolution_convert_fusion.qvis_ref, bf16[2048,128]{1,0:T(8,128)(2,1)} %bitcast.48, bf16[2048,128]{1,0:T(8,128)(2,1)} %bitcast.52, bf16[2048,128]{1,0:T(8,128)(2,1)} %bitcast.51, bf16[64,2048]{1,0:T(8,128)(2,1)} %fusion.12.kh_ref), custom_call_target="tpu_custom_call" | custom-call | flops 2684354560 | bytes 4194304 | tf_op jit(solution)/shard_map/pallas_call | solution.py:77
  67.2 12.6 %all-gather.7.cloned.1.call-done = bf16[8224,128]{1,0:T(8,128)(2,1)} async-done(((bf16[2056,128]{1,0:T(8,128)(2,1)}), bf16[8224,128]{1,0:T(8,128)(2,1)}) %all-gather.7.cloned.1.call-update) | async-done | bytes 2105360 | tf_op jit(solution)/shard_map/all_gather | solution.py:214
  79.8 0.7 convert_bitcast_fusion
  80.5 0.9 fusion.10.kh_ref
  81.4 30.9 %all-gather.5.cloned.1.call-done = bf16[8224,128]{1,0:T(8,128)(2,1)} async-done(((bf16[2056,128]{1,0:T(8,128)(2,1)}), bf16[8224,128]{1,0:T(8,128)(2,1)}) %all-gather.5.cloned.1.call-update) | async-done | bytes 2105360 | tf_op jit(solution)/shard_map/all_gather | solution.py:214
  112.3 0.7 convert_bitcast_fusion.1
  113.0 0.9 fusion.9.kh_ref
  113.9 17.1 %shard_map.74 = (f32[2048,128]{1,0:T(8,128)}, f32[2048,128]{1,0:T(8,128)}, f32[2048,128]{1,0:T(8,128)}) custom-call(s32[1]{0:T(128)} %bitcast.own_ref, bf16[2048,64]{1,0:T(8,128)(2,1)} %convolution_convert_fusion.qvis_ref, bf16[2048,128]{1,0:T(8,128)(2,1)} %bitcast.49, bf16[4,2056,128]{2,1,0:T(8,128)(2,1)} %bitcast.59, bf16[4,2056,128]{2,1,0:T(8,128)(2,1)} %bitcast.60, ...), custom_call_target="tpu_custom_call" | custom-call | flops 4026531840 | bytes 5251072 | tf_op jit(solution)/shard_map/pallas_call | solution.py:146
  131.1 17.4 %shard_map.75 = bf16[2048,128]{1,0:T(8,128)(2,1)} custom-call(s32[1]{0:T(128)} %bitcast.own_ref, bf16[2048,64]{1,0:T(8,128)(2,1)} %convolution_convert_fusion.qvis_ref, bf16[2048,128]{1,0:T(8,128)(2,1)} %bitcast.50, bf16[4,2056,128]{2,1,0:T(8,128)(2,1)} %bitcast.62, bf16[4,2056,128]{2,1,0:T(8,128)(2,1)} %bitcast.63, bf16[4,64,1024]{2,1,0:T(8,128)(2,1)} %fusion.9.kh_ref, ...), custom_call_target="tpu_custom_call" | custom-call | flops 4026531840 | bytes 5251072 | tf_op jit(solution)/shard_map/pallas_call | solution.py:146
  148.4 14.6 %all_to_all.16 = bf16[4,512,128]{2,1,0:T(8,128)(2,1)S(1)} all-to-all(bf16[4,512,128]{2,1,0:T(8,128)(2,1)} %bitcast.47), channel_id=1, replica_groups=mesh['x'=4,'yc'=4,'head'=8] {'yc'}, dimensions={0} | all-to-all | bytes 1048576 | tf_op jit(solution)/shard_map/all_to_all | solution.py:221
  163.1 4.7 %bitcast_convert_fusion = bf16[512,4096]{1,0:T(8,128)(2,1)S(1)} fusion(bf16[4,512,128]{2,1,0:T(8,128)(2,1)S(1)} %all_to_all.16, bf16[4,128,4096]{2,1,0:T(8,128)(2,1)} %param.9), kind=kOutput, calls=%fused_computation.2 | convolution fusion | flops 2149580800 | bytes 8912896 | tf_op jit(solution)/shard_map/hrd,hdo->ro/dot_general | solution.py:222
  167.8 53.5 %all_to_all.17 = bf16[8,64,4096]{2,1,0:T(8,128)(2,1)} all-to-all(bf16[8,64,4096]{2,1,0:T(8,128)(2,1)S(1)} %bitcast.42), channel_id=1, replica_groups=mesh['x'=4,'yc'=4,'head'=8] {'head'}, dimensions={0} | all-to-all | bytes 8388608 | tf_op jit(solution)/shard_map/all_to_all | solution.py:227
  221.3 3.8 %reduce_sum.22 = bf16[64,4096]{1,0:T(8,128)(2,1)} reduce(bf16[8,64,4096]{2,1,0:T(8,128)(2,1)} %all_to_all.17, bf16[]{:T(256)} %constant.13.clone.1), dimensions={0}, to_apply=%region_1.2 | reduce | flops 1835008 | bytes 4718594 | tf_op jit(solution)/shard_map/reduce_sum | solution.py:228
  (17 shorter events, 0.4 us)
Async XLA Ops:
  6.5 1.5 copy-start
  6.5 73.3 %all-gather.7.cloned.1.call-start = ((), (), s32[]{:S(2)}) async-start(), calls=%async_computation.4 | async-start | bytes 2631680 | tf_op jit(solution)/shard_map/all_gather | solution.py:214
  49.9 2.1 copy-start.1
  50.9 61.5 %all-gather.5.cloned.1.call-start = ((), (), s32[]{:S(2)}) async-start(), calls=%async_computation.3 | async-start | bytes 2631680 | tf_op jit(solution)/shard_map/all_gather | solution.py:214
Sparse Core Ops, SparseCore 0:
  51.0 28.7 all-gather.6
  81.5 30.8 all-gather.4
where the time goes:
time: 234 us; the launch traced here: 232 us
  blocking collectives  94 us (40%)
  Pallas kernels  46.1 us (20%)
  waiting for transfers between devices  43.6 us (19%)
  matrix products  21.9 us (9%)
  between operations  13.5 us (6%)
  other arithmetic  11.1 us (5%)
    all_to_all x1, blocking collectives, per_device_body(): parts = lax.all_to_all(parts, 'head', 0, 0)  53.5 us
    all_gather x2, waiting for transfers between devices, per_device_body(): gathered.append(lax.all_gather(payloads[i], 'x', axis=0))  43.5 us
    pallas_call x2, Pallas kernels, attend_remote(): pl.pallas_call(kernel, grid_spec=grid_spec, out_shape=out_shape, compiler...  34.5 us
    all_to_all x1, blocking collectives, per_device_body(): exch = lax.all_to_all(payload, 'yc', 0, 0, tiled=True)  25.9 us
    all_to_all x1, blocking collectives, per_device_body(): lax.all_to_all(attended.reshape(heads_here, tok, lane), 'yc', 0, 0, tiled...  14.6 us
    pallas_call x1, Pallas kernels, attend_local(): pl.pallas_call(functools.partial(local_kernel, scale=scale), grid=(nsteps...  11.6 us
    dot_general x1, matrix products, per_device_body(): jnp.einsum('td,dchk->hctk', moduled, qkv_weight, preferred_element_type=j...  10 us
    dot_general x1, matrix products, per_device_body(): modulation = jnp.dot(level_hot, mod_table, precision=lax.Precision.HIGHEST)  5.59 us
  transfers between devices with their start and end apart: 2, of which 2 were waited for; matrix products, arithmetic and copies ran while one was open for 3% of the time, Pallas kernels for 5%

commit v1 on v0

--- a/solution.py
+++ b/solution.py
@@ -188,21 +188,21 @@
     keys = exch[:, tok:2 * tok].reshape(group_tok, lane)
     values = exch[:, 2 * tok:3 * tok].reshape(group_tok, lane)
     clip_group = exch[:, 3 * tok:3 * tok + clip_rows].reshape(group_tok)
-    halves = 2
-    half_tok = group_tok // halves
-    half_rows = half_tok // lane
-    kv_pad = -half_rows % 8
-    payloads = [
-        jnp.concatenate(
-            [
-                keys[i * half_tok:(i + 1) * half_tok],
-                values[i * half_tok:(i + 1) * half_tok],
-                clip_group[i * half_tok:(i + 1) * half_tok].reshape(half_rows, lane),
-                jnp.zeros((kv_pad, lane), jnp.bfloat16),
-            ]
+    sizes = [3 * group_tok // 4, group_tok // 4]
+    starts = [0, sizes[0]]
+    payloads = []
+    for first, size in zip(starts, sizes):
+        rows = size // lane
+        payloads.append(
+            jnp.concatenate(
+                [
+                    keys[first:first + size],
+                    values[first:first + size],
+                    clip_group[first:first + size].reshape(rows, lane),
+                    jnp.zeros((-rows % 8, lane), jnp.bfloat16),
+                ]
+            )
         )
-        for i in range(halves)
-    ]
     query_hot = (clip_group.astype(jnp.int32)[:, None] == clip_ids).astype(jnp.float32)
     qvis = jnp.dot(query_hot, visible.astype(jnp.float32), precision=lax.Precision.HIGHEST).astype(jnp.bfloat16)
     score_scale = float(np.float32(1.0) / np.sqrt(np.float32(head_size)) * np.float32(math.log2(math.e)))
@@ -210,13 +210,14 @@
     carry = attend_local(qvis, queries, keys, values, local_hot, score_scale)
     own = lax.axis_index("x").reshape(1).astype(jnp.int32)
     gathered = []
-    for i in range(halves):
+    for i in range(len(sizes)):
         gathered.append(lax.all_gather(payloads[i], "x", axis=0))
-    for i in range(halves):
+    for i, size in enumerate(sizes):
         kv_all = gathered[i]
-        key_clips = kv_all[:, 2 * half_tok:2 * half_tok + half_rows].reshape(kv_all.shape[0], half_tok)
+        rows = size // lane
+        key_clips = kv_all[:, 2 * size:2 * size + rows].reshape(kv_all.shape[0], size)
         key_hot = (key_clips.astype(jnp.int32)[:, None, :] == clip_ids[0][None, :, None]).astype(jnp.bfloat16)
-        carry = attend_remote(own, qvis, queries, kv_all, key_hot, carry, score_scale, half_tok, i == halves - 1)
+        carry = attend_remote(own, qvis, queries, kv_all, key_hot, carry, score_scale, size, i == len(sizes) - 1)
     attended = carry
     back = lax.all_to_all(attended.reshape(heads_here, tok, lane), "yc", 0, 0, tiled=True)
     mixed = jnp.einsum(

time: 234 us -> 240 us (1.026)
  local copies, waits for them, and re-layouts: 1.48 us -> 7.99 us
    concatenate x0 -> x2, local copies, waits for them, and re-layouts: none -> 6.52 us  [per_device_body(): jnp.concatenate([keys[first:first + size], values[first:first + size], cl...]
  transfers between devices with their start and end apart: 2 -> 2, of which waited for: 2 -> 2; matrix products, arithmetic and copies ran while one was open for 3% -> 4% of each run, Pallas kernels for 5% -> 5%
where the time goes in v1:
time: 240 us; the launch traced here: 237 us
  blocking collectives  94.1 us (39%)
  Pallas kernels  47.7 us (20%)
  waiting for transfers between devices  42.3 us (18%)
  matrix products  21.9 us (9%)
  between operations  13.5 us (6%)
  other arithmetic  9.4 us (4%)
  local copies, waits for them, and re-layouts  7.99 us (3%)
    all_to_all x1, blocking collectives, per_device_body(): parts = lax.all_to_all(parts, 'head', 0, 0)  53.4 us
    all_gather x2, waiting for transfers between devices, per_device_body(): gathered.append(lax.all_gather(payloads[i], 'x', axis=0))  42.3 us
    pallas_call x2, Pallas kernels, attend_remote(): pl.pallas_call(kernel, grid_spec=grid_spec, out_shape=out_shape, compiler...  36 us
    all_to_all x1, blocking collectives, per_device_body(): exch = lax.all_to_all(payload, 'yc', 0, 0, tiled=True)  25.9 us
    all_to_all x1, blocking collectives, per_device_body(): lax.all_to_all(attended.reshape(heads_here, tok, lane), 'yc', 0, 0, tiled...  14.7 us
    pallas_call x1, Pallas kernels, attend_local(): pl.pallas_call(functools.partial(local_kernel, scale=scale), grid=(nsteps...  11.7 us
    dot_general x1, matrix products, per_device_body(): jnp.einsum('td,dchk->hctk', moduled, qkv_weight, preferred_element_type=j...  10 us
    concatenate x2, local copies, waits for them, and re-layouts, per_device_body(): jnp.concatenate([keys[first:first + size], values[first:first + size], cl...  6.52 us
  transfers between devices with their start and end apart: 2, of which 2 were waited for; matrix products, arithmetic and copies ran while one was open for 4% of the time, Pallas kernels for 5%

profile of v1, /device:TPU:6, one launch (start us, length us, event | category | flops | bytes accessed | tf_op | source)
XLA Modules:
  0.0 237.2 jit_solution(9466379979216247474)
XLA Ops:
  6.5 0.7 convert_bitcast_fusion.2
  7.3 0.8 select_reduce_fusion
  8.1 5.6 %fusion.2 = bf16[512,4096,1,1]{1,0,3,2:T(8,128)(2,1)S(1)} fusion(f32[16,4096]{1,0:T(8,128)S(1)} %copy-done, bf16[512,4096]{1,0:T(8,128)(2,1)} %param.7, s32[512]{0:T(512)S(1)} %select_reduce_fusion), kind=kOutput, calls=%fused_computation.4 | convolution fusion | flops 411049984 | bytes 8652800 | tf_op jit(solution)/shard_map/dot_general | solution.py:170
  13.7 10.0 %fusion.7 = bf16[4,3,512,128]{3,2,0,1:T(8,128)(2,1)S(1)} fusion(bf16[512,4096,1,1]{1,0,3,2:T(8,128)(2,1)S(1)} %fusion.2, bf16[4096,3,4,128]{3,2,1,0:T(4,128)(2,1)} %param.8), kind=kOutput, calls=%fused_computation.10 | convolution fusion | flops 6443237376 | bytes 18350080 | tf_op jit(solution)/shard_map/td,dchk->hctk/dot_general | solution.py:172
  24.0 25.9 %all_to_all.15 = bf16[4,1544,128]{2,1,0:T(8,128)(2,1)S(1)} all-to-all(bf16[4,1544,128]{2,1,0:T(8,128)(2,1)S(1)} %pad_maximum_fusion), channel_id=1, replica_groups=mesh['x'=4,'yc'=4,'head'=8] {'yc'}, dimensions={0} | all-to-all | bytes 3162112 | tf_op jit(solution)/shard_map/all_to_all | solution.py:185
  49.9 2.0 concatenate.14
  51.9 0.2 all-gather.7.cloned.1.call-start
  52.2 4.5 %concatenate.15 = bf16[3088,128]{1,0:T(8,128)(2,1)} concatenate(bf16[1536,128]{1,0:T(8,128)(2,1)S(1)} %bitcast.46, bf16[1536,128]{1,0:T(8,128)(2,1)S(1)} %bitcast.45, bf16[12,128]{1,0:T(8,128)(2,1)S(1)} %reshape.75, bf16[4,128]{1,0:T(4,128)(2,1)S(1)} %broadcast.8), dimensions={0} | concatenate | bytes 1581056 | tf_op jit(solution)/shard_map/concatenate | solution.py:197
  56.9 1.5 convolution_convert_fusion.qvis_ref
  58.4 1.2 fusion.15
  59.6 0.7 fusion.12.kh_ref
  60.3 11.7 %shard_map.73 = (f32[2048,128]{1,0:T(8,128)}, f32[2048,128]{1,0:T(8,128)}, f32[2048,128]{1,0:T(8,128)}) custom-call(bf16[2048,64]{1,0:T(8,128)(2,1)} %convolution_convert_fusion.qvis_ref, bf16[2048,128]{1,0:T(8,128)(2,1)} %bitcast.48, bf16[2048,128]{1,0:T(8,128)(2,1)} %bitcast.52, bf16[2048,128]{1,0:T(8,128)(2,1)} %bitcast.51, bf16[64,2048]{1,0:T(8,128)(2,1)} %fusion.12.kh_ref), custom_call_target="tpu_custom_call" | custom-call | flops 2684354560 | bytes 4194304 | tf_op jit(solution)/shard_map/pallas_call | solution.py:77
  72.0 2.8 %all-gather.5.cloned.1.call-done = bf16[4128,128]{1,0:T(8,128)(2,1)} async-done(((bf16[1032,128]{1,0:T(8,128)(2,1)}), bf16[4128,128]{1,0:T(8,128)(2,1)}) %all-gather.5.cloned.1.call-update) | async-done | bytes 1056784 | tf_op jit(solution)/shard_map/all_gather | solution.py:214
  74.8 0.7 convert_bitcast_fusion.1
  75.5 0.7 fusion.11.kh_ref
  76.3 39.5 %all-gather.7.cloned.1.call-done = bf16[12352,128]{1,0:T(8,128)(2,1)} async-done(((bf16[3088,128]{1,0:T(8,128)(2,1)}), bf16[12352,128]{1,0:T(8,128)(2,1)}) %all-gather.7.cloned.1.call-update) | async-done | bytes 3162128 | tf_op jit(solution)/shard_map/all_gather | solution.py:214
  115.8 0.7 convert_bitcast_fusion
  116.5 1.0 fusion.6.kh_ref
  117.5 25.4 %shard_map.74 = (f32[2048,128]{1,0:T(8,128)}, f32[2048,128]{1,0:T(8,128)}, f32[2048,128]{1,0:T(8,128)}) custom-call(s32[1]{0:T(128)} %bitcast.own_ref, bf16[2048,64]{1,0:T(8,128)(2,1)} %convolution_convert_fusion.qvis_ref, bf16[2048,128]{1,0:T(8,128)(2,1)} %bitcast.49, bf16[4,3088,128]{2,1,0:T(8,128)(2,1)} %bitcast.57, bf16[4,3088,128]{2,1,0:T(8,128)(2,1)} %bitcast.58, ...), custom_call_target="tpu_custom_call" | custom-call | flops 6039797760 | bytes 6307840 | tf_op jit(solution)/shard_map/pallas_call | solution.py:146
  142.9 10.6 %shard_map.75 = bf16[2048,128]{1,0:T(8,128)(2,1)} custom-call(s32[1]{0:T(128)} %bitcast.own_ref, bf16[2048,64]{1,0:T(8,128)(2,1)} %convolution_convert_fusion.qvis_ref, bf16[2048,128]{1,0:T(8,128)(2,1)} %bitcast.50, bf16[4,1032,128]{2,1,0:T(8,128)(2,1)} %bitcast.60, bf16[4,1032,128]{2,1,0:T(8,128)(2,1)} %bitcast.61, bf16[4,64,512]{2,1,0:T(8,128)(2,1)} %fusion.11.kh_ref, ...), custom_call_target="tpu_custom_call" | custom-call | flops 2013265920 | bytes 4202496 | tf_op jit(solution)/shard_map/pallas_call | solution.py:146
  153.6 14.7 %all_to_all.16 = bf16[4,512,128]{2,1,0:T(8,128)(2,1)S(1)} all-to-all(bf16[4,512,128]{2,1,0:T(8,128)(2,1)} %bitcast.47), channel_id=1, replica_groups=mesh['x'=4,'yc'=4,'head'=8] {'yc'}, dimensions={0} | all-to-all | bytes 1048576 | tf_op jit(solution)/shard_map/all_to_all | solution.py:222
  168.3 4.7 %bitcast_convert_fusion = bf16[512,4096]{1,0:T(8,128)(2,1)S(1)} fusion(bf16[4,512,128]{2,1,0:T(8,128)(2,1)S(1)} %all_to_all.16, bf16[4,128,4096]{2,1,0:T(8,128)(2,1)} %param.9), kind=kOutput, calls=%fused_computation.2 | convolution fusion | flops 2149580800 | bytes 8912896 | tf_op jit(solution)/shard_map/hrd,hdo->ro/dot_general | solution.py:223
  173.0 53.4 %all_to_all.17 = bf16[8,64,4096]{2,1,0:T(8,128)(2,1)} all-to-all(bf16[8,64,4096]{2,1,0:T(8,128)(2,1)S(1)} %bitcast.44), channel_id=1, replica_groups=mesh['x'=4,'yc'=4,'head'=8] {'head'}, dimensions={0} | all-to-all | bytes 8388608 | tf_op jit(solution)/shard_map/all_to_all | solution.py:228
  226.5 3.8 %reduce_sum.22 = bf16[64,4096]{1,0:T(8,128)(2,1)} reduce(bf16[8,64,4096]{2,1,0:T(8,128)(2,1)} %all_to_all.17, bf16[]{:T(256)} %constant.13.clone.1), dimensions={0}, to_apply=%region_1.2 | reduce | flops 1835008 | bytes 4718594 | tf_op jit(solution)/shard_map/reduce_sum | solution.py:229
  (21 shorter events, 0.4 us)
Async XLA Ops:
  6.5 1.5 copy-start
  6.5 68.3 %all-gather.5.cloned.1.call-start = ((), (), s32[]{:S(2)}) async-start(), calls=%async_computation.3 | async-start | bytes 1320960 | tf_op jit(solution)/shard_map/all_gather | solution.py:214
  24.0 32.9 %copy-start.1 = (s32[64,64]{1,0:T(8,128)S(1)}, s32[64,64]{1,0:T(8,128)}, u32[]{:S(2)}) copy-start(s32[64,64]{1,0:T(8,128)} %param.13) | copy-start | bytes 49156
  51.9 63.9 %all-gather.7.cloned.1.call-start = ((), (), s32[]{:S(2)}) async-start(), calls=%async_computation.4 | async-start | bytes 3952640 | tf_op jit(solution)/shard_map/all_gather | solution.py:214
Sparse Core Ops, SparseCore 0:
  52.0 22.7 all-gather.4
  76.5 39.2 all-gather.6

commit v2 on v0

--- a/solution.py
+++ b/solution.py
@@ -178,16 +178,18 @@
     clip_slab = jnp.concatenate(
         [clip_of.astype(jnp.bfloat16).reshape(clip_rows, lane), jnp.zeros((pad_rows, lane), jnp.bfloat16)]
     )
-    payload = jnp.concatenate(
-        [qkv.reshape(heads_here, 3 * tok, lane), jnp.broadcast_to(clip_slab, (heads_here,) + clip_slab.shape)],
+    kv_part = jnp.concatenate(
+        [qkv[:, 1:3].reshape(heads_here, 2 * tok, lane), jnp.broadcast_to(clip_slab, (heads_here,) + clip_slab.shape)],
         axis=1,
     )
-    exch = lax.all_to_all(payload, "yc", 0, 0, tiled=True)
+    exch = lax.all_to_all(kv_part, "yc", 0, 0, tiled=True)
+    q_part, exch = lax.optimization_barrier((qkv[:, 0], exch))
+    exch_q = lax.all_to_all(q_part, "yc", 0, 0, tiled=True)
     group_tok = heads_here * tok
-    queries = exch[:, 0:tok].reshape(group_tok, lane)
-    keys = exch[:, tok:2 * tok].reshape(group_tok, lane)
-    values = exch[:, 2 * tok:3 * tok].reshape(group_tok, lane)
-    clip_group = exch[:, 3 * tok:3 * tok + clip_rows].reshape(group_tok)
+    queries = exch_q.reshape(group_tok, lane)
+    keys = exch[:, 0:tok].reshape(group_tok, lane)
+    values = exch[:, tok:2 * tok].reshape(group_tok, lane)
+    clip_group = exch[:, 2 * tok:2 * tok + clip_rows].reshape(group_tok)
     halves = 2
     half_tok = group_tok // halves
     half_rows = half_tok // lane

time: 234 us -> 230 us (0.983)
  blocking collectives: 94 us -> 68 us
  waiting for transfers between devices: 43.6 us -> 54.5 us
  starting transfers between devices: 0.22 us -> 8.17 us
    all_to_all x1 -> x0, blocking collectives: 25.9 us -> none  [per_device_body(): exch = lax.all_to_all(payload, 'yc', 0, 0, tiled=True)]
    all_to_all x0 -> x2, waiting for transfers between devices: none -> 21.9 us  [the longest x1 15.2 us: per_device_body(): exch = lax.all_to_all(kv_part, 'yc', 0, 0, tiled=True)]
    all_gather x2, waiting for transfers between devices: 43.5 us -> 32.7 us  [per_device_body(): gathered.append(lax.all_gather(payloads[i], 'x', axis=0))]
    all_to_all x0 -> x2, starting transfers between devices: none -> 8.13 us  [the longest x1 4.47 us: per_device_body(): exch = lax.all_to_all(kv_part, 'yc', 0, 0, tiled=True)]
  transfers between devices with their start and end apart: 2 -> 4, of which waited for: 2 -> 4; matrix products, arithmetic and copies ran while one was open for 3% -> 3% of each run, Pallas kernels for 5% -> 5%
where the time goes in v2:
time: 230 us; the launch traced here: 227 us
  blocking collectives  68 us (30%)
  waiting for transfers between devices  54.5 us (24%)
  Pallas kernels  46.2 us (20%)
  matrix products  21.9 us (10%)
  between operations  13.5 us (6%)
  other arithmetic  12.1 us (5%)
  starting transfers between devices  8.17 us (4%)
  local copies, waits for them, and re-layouts  3.03 us (1%)
    all_to_all x1, blocking collectives, per_device_body(): parts = lax.all_to_all(parts, 'head', 0, 0)  53.4 us
    pallas_call x2, Pallas kernels, attend_remote(): pl.pallas_call(kernel, grid_spec=grid_spec, out_shape=out_shape, compiler...  34.5 us
    all_gather x2, waiting for transfers between devices, per_device_body(): gathered.append(lax.all_gather(payloads[i], 'x', axis=0))  32.7 us
    all_to_all x1, waiting for transfers between devices, per_device_body(): exch = lax.all_to_all(kv_part, 'yc', 0, 0, tiled=True)  15.2 us
    all_to_all x1, blocking collectives, per_device_body(): lax.all_to_all(attended.reshape(heads_here, tok, lane), 'yc', 0, 0, tiled...  14.6 us
    pallas_call x1, Pallas kernels, attend_local(): pl.pallas_call(functools.partial(local_kernel, scale=scale), grid=(nsteps...  11.7 us
    dot_general x1, matrix products, per_device_body(): jnp.einsum('td,dchk->hctk', moduled, qkv_weight, preferred_element_type=j...  10 us
    all_to_all x1, waiting for transfers between devices, per_device_body(): exch_q = lax.all_to_all(q_part, 'yc', 0, 0, tiled=True)  6.67 us
  transfers between devices with their start and end apart: 4, of which 4 were waited for; matrix products, arithmetic and copies ran while one was open for 3% of the time, Pallas kernels for 5%

profile of v2, /device:TPU:6, one launch (start us, length us, event | category | flops | bytes accessed | tf_op | source)
XLA Modules:
  0.0 227.5 jit_solution(2723340073772032342)
XLA Ops:
  8.1 5.6 %fusion.2 = bf16[512,4096,1,1]{1,0,3,2:T(8,128)(2,1)S(1)} fusion(f32[16,4096]{1,0:T(8,128)S(1)} %copy-done, bf16[512,4096]{1,0:T(8,128)(2,1)} %param.7, s32[512]{0:T(512)S(1)} %select_reduce_fusion), kind=kOutput, calls=%fused_computation.4 | convolution fusion | flops 411049984 | bytes 8652800 | tf_op jit(solution)/shard_map/dot_general | solution.py:170
  13.7 10.0 %fusion.6 = bf16[4,3,512,128]{3,2,0,1:T(8,128)(2,1)S(1)} fusion(bf16[512,4096,1,1]{1,0,3,2:T(8,128)(2,1)S(1)} %fusion.2, bf16[4096,3,4,128]{3,2,1,0:T(4,128)(2,1)} %param.8), kind=kOutput, calls=%fused_computation.7 | convolution fusion | flops 6443237376 | bytes 18350080 | tf_op jit(solution)/shard_map/td,dchk->hctk/dot_general | solution.py:172
  23.9 1.0 pad_maximum_fusion
  24.9 4.5 %all-to-all-start = ((bf16[4,1032,128]{2,1,0:T(8,128)(2,1)}), bf16[4,1032,128]{2,1,0:T(8,128)(2,1)S(1)}, u32[]{:S(2)}, u32[]{:S(2)}) async-start(bf16[4,1032,128]{2,1,0:T(8,128)(2,1)} %pad_maximum_fusion), calls=%async_computation | async-start | bytes 2113536 | tf_op jit(solution)/shard_map/all_to_all | solution.py:185
  29.4 0.8 slice_bitcast_fusion
  30.2 15.2 %all-to-all-done = bf16[4,1032,128]{2,1,0:T(8,128)(2,1)S(1)} async-done(((bf16[4,1032,128]{2,1,0:T(8,128)(2,1)}), bf16[4,1032,128]{2,1,0:T(8,128)(2,1)S(1)}, u32[]{:S(2)}, u32[]{:S(2)}) %all-to-all-start) | async-done | bytes 1056800 | tf_op jit(solution)/shard_map/all_to_all | solution.py:185
  45.5 0.9 pad_maximum_fusion.2
  46.5 0.8 pad_maximum_fusion.1
  47.4 3.7 %all-to-all-start.1 = ((bf16[4,512,128]{2,1,0:T(8,128)(2,1)}), bf16[4,512,128]{2,1,0:T(8,128)(2,1)S(1)}, u32[]{:S(2)}, u32[]{:S(2)}) async-start(bf16[4,512,128]{2,1,0:T(8,128)(2,1)} %slice_bitcast_fusion), calls=%async_computation.1 | async-start | bytes 1048576 | tf_op jit(solution)/shard_map/all_to_all | solution.py:187
  51.0 1.5 convolution_convert_fusion.qvis_ref
  52.6 1.1 fusion.15
  54.5 6.7 %all-to-all-done.1 = bf16[4,512,128]{2,1,0:T(8,128)(2,1)S(1)} async-done(((bf16[4,512,128]{2,1,0:T(8,128)(2,1)}), bf16[4,512,128]{2,1,0:T(8,128)(2,1)S(1)}, u32[]{:S(2)}, u32[]{:S(2)}) %all-to-all-start.1) | async-done | bytes 524320 | tf_op jit(solution)/shard_map/all_to_all | solution.py:187
  61.1 0.8 copy-done.1
  61.9 11.7 %shard_map.73 = (f32[2048,128]{1,0:T(8,128)}, f32[2048,128]{1,0:T(8,128)}, f32[2048,128]{1,0:T(8,128)}) custom-call(bf16[2048,64]{1,0:T(8,128)(2,1)} %convolution_convert_fusion.qvis_ref, bf16[2048,128]{1,0:T(8,128)(2,1)} %bitcast.49, bf16[2048,128]{1,0:T(8,128)(2,1)} %bitcast.54, bf16[2048,128]{1,0:T(8,128)(2,1)} %bitcast.53, bf16[64,2048]{1,0:T(8,128)(2,1)} %fusion.12.kh_ref), custom_call_target="tpu_custom_call" | custom-call | flops 2684354560 | bytes 4194304 | tf_op jit(solution)/shard_map/pallas_call | solution.py:77
  73.6 1.7 all-gather.7.cloned.1.call-done
  76.1 0.9 fusion.10.kh_ref
  77.0 30.9 %all-gather.5.cloned.1.call-done = bf16[8224,128]{1,0:T(8,128)(2,1)} async-done(((bf16[2056,128]{1,0:T(8,128)(2,1)}), bf16[8224,128]{1,0:T(8,128)(2,1)}) %all-gather.5.cloned.1.call-update) | async-done | bytes 2105360 | tf_op jit(solution)/shard_map/all_gather | solution.py:216
  108.6 0.9 fusion.9.kh_ref
  109.5 17.1 %shard_map.74 = (f32[2048,128]{1,0:T(8,128)}, f32[2048,128]{1,0:T(8,128)}, f32[2048,128]{1,0:T(8,128)}) custom-call(s32[1]{0:T(128)} %bitcast.own_ref, bf16[2048,64]{1,0:T(8,128)(2,1)} %convolution_convert_fusion.qvis_ref, bf16[2048,128]{1,0:T(8,128)(2,1)} %bitcast.50, bf16[4,2056,128]{2,1,0:T(8,128)(2,1)} %bitcast.61, bf16[4,2056,128]{2,1,0:T(8,128)(2,1)} %bitcast.62, ...), custom_call_target="tpu_custom_call" | custom-call | flops 4026531840 | bytes 5251072 | tf_op jit(solution)/shard_map/pallas_call | solution.py:146
  126.6 17.4 %shard_map.75 = bf16[2048,128]{1,0:T(8,128)(2,1)} custom-call(s32[1]{0:T(128)} %bitcast.own_ref, bf16[2048,64]{1,0:T(8,128)(2,1)} %convolution_convert_fusion.qvis_ref, bf16[2048,128]{1,0:T(8,128)(2,1)} %bitcast.51, bf16[4,2056,128]{2,1,0:T(8,128)(2,1)} %bitcast.64, bf16[4,2056,128]{2,1,0:T(8,128)(2,1)} %bitcast.65, bf16[4,64,1024]{2,1,0:T(8,128)(2,1)} %fusion.9.kh_ref, ...), custom_call_target="tpu_custom_call" | custom-call | flops 4026531840 | bytes 5251072 | tf_op jit(solution)/shard_map/pallas_call | solution.py:146
  144.0 14.6 %all_to_all.20 = bf16[4,512,128]{2,1,0:T(8,128)(2,1)S(1)} all-to-all(bf16[4,512,128]{2,1,0:T(8,128)(2,1)} %bitcast.52), channel_id=1, replica_groups=mesh['x'=4,'yc'=4,'head'=8] {'yc'}, dimensions={0} | all-to-all | bytes 1048576 | tf_op jit(solution)/shard_map/all_to_all | solution.py:223
  158.6 4.7 %bitcast_convert_fusion = bf16[512,4096]{1,0:T(8,128)(2,1)S(1)} fusion(bf16[4,512,128]{2,1,0:T(8,128)(2,1)S(1)} %all_to_all.20, bf16[4,128,4096]{2,1,0:T(8,128)(2,1)} %param.9), kind=kOutput, calls=%fused_computation.2 | convolution fusion | flops 2149580800 | bytes 8912896 | tf_op jit(solution)/shard_map/hrd,hdo->ro/dot_general | solution.py:224
  163.3 53.4 %all_to_all.21 = bf16[8,64,4096]{2,1,0:T(8,128)(2,1)} all-to-all(bf16[8,64,4096]{2,1,0:T(8,128)(2,1)S(1)} %bitcast.43), channel_id=1, replica_groups=mesh['x'=4,'yc'=4,'head'=8] {'head'}, dimensions={0} | all-to-all | bytes 8388608 | tf_op jit(solution)/shard_map/all_to_all | solution.py:229
  216.8 3.8 %reduce_sum.22 = bf16[64,4096]{1,0:T(8,128)(2,1)} reduce(bf16[8,64,4096]{2,1,0:T(8,128)(2,1)} %all_to_all.21, bf16[]{:T(256)} %constant.13.clone.1), dimensions={0}, to_apply=%region_1.2 | reduce | flops 1835008 | bytes 4718594 | tf_op jit(solution)/shard_map/reduce_sum | solution.py:230
  (24 shorter events, 4.0 us)
Async XLA Ops:
  6.5 1.5 copy-start
  24.9 20.5 %all-to-all-start = ((bf16[4,1032,128]{2,1,0:T(8,128)(2,1)}), bf16[4,1032,128]{2,1,0:T(8,128)(2,1)S(1)}, u32[]{:S(2)}, u32[]{:S(2)}) async-start(bf16[4,1032,128]{2,1,0:T(8,128)(2,1)} %pad_maximum_fusion), calls=%async_computation | async-start | bytes 2113536 | tf_op jit(solution)/shard_map/all_to_all | solution.py:185
  29.4 45.9 %all-gather.7.cloned.1.call-start = ((), (), s32[]{:S(2)}) async-start(), calls=%async_computation.5 | async-start | bytes 2631680 | tf_op jit(solution)/shard_map/all_gather | solution.py:216
  45.5 5.5 %copy-start.2 = (s32[64,64]{1,0:T(8,128)S(1)}, s32[64,64]{1,0:T(8,128)}, u32[]{:S(2)}) copy-start(s32[64,64]{1,0:T(8,128)} %param.13) | copy-start | bytes 49156
  46.4 61.5 %all-gather.5.cloned.1.call-start = ((), (), s32[]{:S(2)}) async-start(), calls=%async_computation.4 | async-start | bytes 2631680 | tf_op jit(solution)/shard_map/all_gather | solution.py:216
  47.4 13.8 %all-to-all-start.1 = ((bf16[4,512,128]{2,1,0:T(8,128)(2,1)}), bf16[4,512,128]{2,1,0:T(8,128)(2,1)S(1)}, u32[]{:S(2)}, u32[]{:S(2)}) async-start(bf16[4,512,128]{2,1,0:T(8,128)(2,1)} %slice_bitcast_fusion), calls=%async_computation.1 | async-start | bytes 1048576 | tf_op jit(solution)/shard_map/all_to_all | solution.py:187
  61.1 0.8 copy-start.1
Sparse Core Ops, SparseCore 0:
  46.5 28.7 all-gather.6
  77.0 30.8 all-gather.4

commit v3 on v2

--- a/solution.py
+++ b/solution.py
@@ -99,16 +99,14 @@
     )(qvis, q, keys, values, key_hot)
 
 
-def attend_remote(own, qvis, q, kv_all, key_hot, carry, scale, tok, finalize):
+def attend_remote(own, qvis, q, kv_all, key_hot, carry, scale, finalize):
     nq, hd = q.shape
-    sources = kv_all.shape[0]
+    sources, blocks, _, bk = key_hot.shape
     clip_count = qvis.shape[1]
-    bk = math.gcd(tok, 1024)
-    sub = tok // bk
-    nsteps = (sources - 1) * sub
+    nsteps = (sources - 1) * blocks
 
     def src(j, o):
-        return (o[0] + 1 + j // sub) % sources
+        return (o[0] + 1 + j // blocks) % sources
 
     state_specs = [
         pl.BlockSpec((nq, 128), lambda j, o: (0, 0)),
@@ -136,22 +134,23 @@
         in_specs=[
             pl.BlockSpec((nq, clip_count), lambda j, o: (0, 0)),
             pl.BlockSpec((nq, hd), lambda j, o: (0, 0)),
-            pl.BlockSpec((None, bk, hd), lambda j, o: (src(j, o), j % sub, 0)),
-            pl.BlockSpec((None, bk, hd), lambda j, o: (src(j, o), sub + j % sub, 0)),
-            pl.BlockSpec((None, clip_count, bk), lambda j, o: (src(j, o), 0, j % sub)),
+            pl.BlockSpec((None, None, bk, hd), lambda j, o: (src(j, o), j % blocks, 0, 0)),
+            pl.BlockSpec((None, None, bk, hd), lambda j, o: (src(j, o), j % blocks, 1, 0)),
+            pl.BlockSpec((None, None, clip_count, bk), lambda j, o: (src(j, o), j % blocks, 0, 0)),
         ] + state_specs,
         out_specs=out_specs,
         scratch_shapes=scratch,
     )
+    keys_seen = (sources - 1) * blocks * bk
     return pl.pallas_call(
         kernel,
         grid_spec=grid_spec,
         out_shape=out_shape,
         compiler_params=pltpu.CompilerParams(dimension_semantics=("arbitrary",)),
         cost_estimate=pl.CostEstimate(
-            flops=4 * nq * (sources - 1) * tok * hd + 2 * nq * clip_count * (sources - 1) * tok,
-            transcendentals=nq * (sources - 1) * tok,
-            bytes_accessed=kv_all.size * 2 + 3 * nq * 512,
+            flops=4 * nq * keys_seen * hd + 2 * nq * clip_count * keys_seen,
+            transcendentals=nq * keys_seen,
+            bytes_accessed=4 * keys_seen * hd + 3 * nq * 512,
         ),
     )(own, qvis, q, kv_all, kv_all, key_hot, *carry)
 
@@ -190,35 +189,21 @@
     keys = exch[:, 0:tok].reshape(group_tok, lane)
     values = exch[:, tok:2 * tok].reshape(group_tok, lane)
     clip_group = exch[:, 2 * tok:2 * tok + clip_rows].reshape(group_tok)
-    halves = 2
-    half_tok = group_tok // halves
-    half_rows = half_tok // lane
-    kv_pad = -half_rows % 8
-    payloads = [
-        jnp.concatenate(
-            [
-                keys[i * half_tok:(i + 1) * half_tok],
-                values[i * half_tok:(i + 1) * half_tok],
-                clip_group[i * half_tok:(i + 1) * half_tok].reshape(half_rows, lane),
-                jnp.zeros((kv_pad, lane), jnp.bfloat16),
-            ]
-        )
-        for i in range(halves)
-    ]
     query_hot = (clip_group.astype(jnp.int32)[:, None] == clip_ids).astype(jnp.float32)
     qvis = jnp.dot(query_hot, visible.astype(jnp.float32), precision=lax.Precision.HIGHEST).astype(jnp.bfloat16)
     score_scale = float(np.float32(1.0) / np.sqrt(np.float32(head_size)) * np.float32(math.log2(math.e)))
     local_hot = (clip_group.astype(jnp.int32)[None, :] == clip_ids[0][:, None]).astype(jnp.bfloat16)
     carry = attend_local(qvis, queries, keys, values, local_hot, score_scale)
     own = lax.axis_index("x").reshape(1).astype(jnp.int32)
+    bounds = [(0, heads_here - 1), (heads_here - 1, heads_here)]
     gathered = []
-    for i in range(halves):
-        gathered.append(lax.all_gather(payloads[i], "x", axis=0))
-    for i in range(halves):
+    for lo, hi in bounds:
+        gathered.append(lax.all_gather(exch[lo:hi], "x", axis=0))
+    for i in range(len(bounds)):
         kv_all = gathered[i]
-        key_clips = kv_all[:, 2 * half_tok:2 * half_tok + half_rows].reshape(kv_all.shape[0], half_tok)
-        key_hot = (key_clips.astype(jnp.int32)[:, None, :] == clip_ids[0][None, :, None]).astype(jnp.bfloat16)
-        carry = attend_remote(own, qvis, queries, kv_all, key_hot, carry, score_scale, half_tok, i == halves - 1)
+        key_clips = kv_all[:, :, 2 * tok:2 * tok + clip_rows].reshape(kv_all.shape[0], kv_all.shape[1], tok)
+        key_hot = (key_clips.astype(jnp.int32)[:, :, None, :] == clip_ids[0][None, None, :, None]).astype(jnp.bfloat16)
+        carry = attend_remote(own, qvis, queries, kv_all, key_hot, carry, score_scale, i == len(bounds) - 1)
     attended = carry
     back = lax.all_to_all(attended.reshape(heads_here, tok, lane), "yc", 0, 0, tiled=True)
     mixed = jnp.einsum(

time: 230 us -> 234 us (1.017)
  waiting for transfers between devices: 54.5 us -> 57.1 us
    all_gather x2, waiting for transfers between devices: 32.7 us -> 35.2 us  [per_device_body(): gathered.append(lax.all_gather(exch[lo:hi], 'x', axis=0))]
  transfers between devices with their start and end apart: 4 -> 4, of which waited for: 4 -> 3; matrix products, arithmetic and copies ran while one was open for 3% -> 3% of each run, Pallas kernels for 5% -> 5%
where the time goes in v3:
time: 234 us; the launch traced here: 232 us
  blocking collectives  68.2 us (29%)
  waiting for transfers between devices  57.1 us (24%)
  Pallas kernels  47.4 us (20%)
  matrix products  21.9 us (9%)
  between operations  13.5 us (6%)
  other arithmetic  10.5 us (4%)
  starting transfers between devices  8.3 us (4%)
  local copies, waits for them, and re-layouts  4.63 us (2%)
    all_to_all x1, blocking collectives, per_device_body(): parts = lax.all_to_all(parts, 'head', 0, 0)  53.5 us
    pallas_call x2, Pallas kernels, attend_remote(): pl.pallas_call(kernel, grid_spec=grid_spec, out_shape=out_shape, compiler...  35.8 us
    all_gather x2, waiting for transfers between devices, per_device_body(): gathered.append(lax.all_gather(exch[lo:hi], 'x', axis=0))  35.2 us
    all_to_all x1, waiting for transfers between devices, per_device_body(): exch = lax.all_to_all(kv_part, 'yc', 0, 0, tiled=True)  15.2 us
    all_to_all x1, blocking collectives, per_device_body(): lax.all_to_all(attended.reshape(heads_here, tok, lane), 'yc', 0, 0, tiled...  14.7 us
    pallas_call x1, Pallas kernels, attend_local(): pl.pallas_call(functools.partial(local_kernel, scale=scale), grid=(nsteps...  11.6 us
    dot_general x1, matrix products, per_device_body(): jnp.einsum('td,dchk->hctk', moduled, qkv_weight, preferred_element_type=j...  10 us
    all_to_all x1, waiting for transfers between devices, per_device_body(): exch_q = lax.all_to_all(q_part, 'yc', 0, 0, tiled=True)  6.64 us
  transfers between devices with their start and end apart: 4, of which 3 were waited for; matrix products, arithmetic and copies ran while one was open for 3% of the time, Pallas kernels for 5%

profile of v3, /device:TPU:6, one launch (start us, length us, event | category | flops | bytes accessed | tf_op | source)
XLA Modules:
  0.0 231.5 jit_solution(13361197515231816153)
XLA Ops:
  7.3 0.8 select_reduce_fusion
  8.1 5.6 %fusion.2 = bf16[512,4096,1,1]{1,0,3,2:T(8,128)(2,1)S(1)} fusion(f32[16,4096]{1,0:T(8,128)S(1)} %copy-done, bf16[512,4096]{1,0:T(8,128)(2,1)} %param.7, s32[512]{0:T(512)S(1)} %select_reduce_fusion), kind=kOutput, calls=%fused_computation.4 | convolution fusion | flops 411049984 | bytes 8652800 | tf_op jit(solution)/shard_map/dot_general | solution.py:169
  13.7 10.0 %fusion.7 = bf16[4,3,512,128]{3,2,0,1:T(8,128)(2,1)S(1)} fusion(bf16[512,4096,1,1]{1,0,3,2:T(8,128)(2,1)S(1)} %fusion.2, bf16[4096,3,4,128]{3,2,1,0:T(4,128)(2,1)} %param.8), kind=kOutput, calls=%fused_computation.9 | convolution fusion | flops 6443237376 | bytes 18350080 | tf_op jit(solution)/shard_map/td,dchk->hctk/dot_general | solution.py:171
  23.9 1.0 pad_maximum_fusion
  24.9 4.6 %all-to-all-start = ((bf16[4,1032,128]{2,1,0:T(8,128)(2,1)}), bf16[4,1032,128]{2,1,0:T(8,128)(2,1)S(1)}, u32[]{:S(2)}, u32[]{:S(2)}) async-start(bf16[4,1032,128]{2,1,0:T(8,128)(2,1)} %pad_maximum_fusion), calls=%async_computation | async-start | bytes 2113536 | tf_op jit(solution)/shard_map/all_to_all | solution.py:184
  29.5 0.8 slice_bitcast_fusion
  30.4 15.2 %all-to-all-done = bf16[4,1032,128]{2,1,0:T(8,128)(2,1)S(1)} async-done(((bf16[4,1032,128]{2,1,0:T(8,128)(2,1)}), bf16[4,1032,128]{2,1,0:T(8,128)(2,1)S(1)}, u32[]{:S(2)}, u32[]{:S(2)}) %all-to-all-start) | async-done | bytes 1056800 | tf_op jit(solution)/shard_map/all_to_all | solution.py:184
  46.4 0.9 slice.32
  47.4 3.7 %all-to-all-start.1 = ((bf16[4,512,128]{2,1,0:T(8,128)(2,1)}), bf16[4,512,128]{2,1,0:T(8,128)(2,1)S(1)}, u32[]{:S(2)}, u32[]{:S(2)}) async-start(bf16[4,512,128]{2,1,0:T(8,128)(2,1)} %slice_bitcast_fusion), calls=%async_computation.1 | async-start | bytes 1048576 | tf_op jit(solution)/shard_map/all_to_all | solution.py:186
  51.0 1.5 convolution_convert_fusion.qvis_ref
  52.6 1.2 fusion.15
  53.7 0.8 fusion.12.kh_ref
  54.5 6.6 %all-to-all-done.1 = bf16[4,512,128]{2,1,0:T(8,128)(2,1)S(1)} async-done(((bf16[4,512,128]{2,1,0:T(8,128)(2,1)}), bf16[4,512,128]{2,1,0:T(8,128)(2,1)S(1)}, u32[]{:S(2)}, u32[]{:S(2)}) %all-to-all-start.1) | async-done | bytes 524320 | tf_op jit(solution)/shard_map/all_to_all | solution.py:186
  61.1 0.8 copy-done.1
  61.9 11.6 %shard_map.73 = (f32[2048,128]{1,0:T(8,128)}, f32[2048,128]{1,0:T(8,128)}, f32[2048,128]{1,0:T(8,128)}) custom-call(bf16[2048,64]{1,0:T(8,128)(2,1)} %convolution_convert_fusion.qvis_ref, bf16[2048,128]{1,0:T(8,128)(2,1)} %bitcast.35, bf16[2048,128]{1,0:T(8,128)(2,1)} %bitcast.40, bf16[2048,128]{1,0:T(8,128)(2,1)} %bitcast.39, bf16[64,2048]{1,0:T(8,128)(2,1)} %fusion.12.kh_ref), custom_call_target="tpu_custom_call" | custom-call | flops 2684354560 | bytes 4194304 | tf_op jit(solution)/shard_map/pallas_call | solution.py:77
  74.3 0.8 fusion.11.kh_ref
  75.0 35.2 %all-gather.7.cloned.1.call-done = bf16[12,1032,128]{2,1,0:T(8,128)(2,1)} async-done(((bf16[3,1032,128]{2,1,0:T(8,128)(2,1)}), bf16[12,1032,128]{2,1,0:T(8,128)(2,1)}) %all-gather.7.cloned.1.call-update) | async-done | bytes 3170320 | tf_op jit(solution)/shard_map/all_gather | solution.py:201
  111.0 1.1 fusion.6.kh_ref
  112.2 25.1 %shard_map.74 = (f32[2048,128]{1,0:T(8,128)}, f32[2048,128]{1,0:T(8,128)}, f32[2048,128]{1,0:T(8,128)}) custom-call(s32[1]{0:T(128)} %bitcast.own_ref, bf16[2048,64]{1,0:T(8,128)(2,1)} %convolution_convert_fusion.qvis_ref, bf16[2048,128]{1,0:T(8,128)(2,1)} %bitcast.36, bf16[4,3,1032,128]{3,2,1,0:T(8,128)(2,1)} %bitcast.44, ...), custom_call_target="tpu_custom_call" | custom-call | flops 6039797760 | bytes 5505024 | tf_op jit(solution)/shard_map/pallas_call | solution.py:145
  137.3 10.6 %shard_map.75 = bf16[2048,128]{1,0:T(8,128)(2,1)} custom-call(s32[1]{0:T(128)} %bitcast.own_ref, bf16[2048,64]{1,0:T(8,128)(2,1)} %convolution_convert_fusion.qvis_ref, bf16[2048,128]{1,0:T(8,128)(2,1)} %bitcast.37, bf16[4,1,1032,128]{3,2,1,0:T(8,128)(2,1)} %bitcast.47, bf16[4,1,1032,128]{3,2,1,0:T(8,128)(2,1)} %bitcast.48, ...), custom_call_target="tpu_custom_call" | custom-call | flops 2013265920 | bytes 3932160 | tf_op jit(solution)/shard_map/pallas_call | solution.py:145
  147.9 14.7 %all_to_all.20 = bf16[4,512,128]{2,1,0:T(8,128)(2,1)S(1)} all-to-all(bf16[4,512,128]{2,1,0:T(8,128)(2,1)} %bitcast.38), channel_id=1, replica_groups=mesh['x'=4,'yc'=4,'head'=8] {'yc'}, dimensions={0} | all-to-all | bytes 1048576 | tf_op jit(solution)/shard_map/all_to_all | solution.py:208
  162.6 4.7 %bitcast_convert_fusion = bf16[512,4096]{1,0:T(8,128)(2,1)S(1)} fusion(bf16[4,512,128]{2,1,0:T(8,128)(2,1)S(1)} %all_to_all.20, bf16[4,128,4096]{2,1,0:T(8,128)(2,1)} %param.9), kind=kOutput, calls=%fused_computation.2 | convolution fusion | flops 2149580800 | bytes 8912896 | tf_op jit(solution)/shard_map/hrd,hdo->ro/dot_general | solution.py:209
  167.4 53.5 %all_to_all.21 = bf16[8,64,4096]{2,1,0:T(8,128)(2,1)} all-to-all(bf16[8,64,4096]{2,1,0:T(8,128)(2,1)S(1)} %bitcast.33), channel_id=1, replica_groups=mesh['x'=4,'yc'=4,'head'=8] {'head'}, dimensions={0} | all-to-all | bytes 8388608 | tf_op jit(solution)/shard_map/all_to_all | solution.py:214
  220.8 3.8 %reduce_sum.22 = bf16[64,4096]{1,0:T(8,128)(2,1)} reduce(bf16[8,64,4096]{2,1,0:T(8,128)(2,1)} %all_to_all.21, bf16[]{:T(256)} %constant.13.clone.1), dimensions={0}, to_apply=%region_1.2 | reduce | flops 1835008 | bytes 4718594 | tf_op jit(solution)/shard_map/reduce_sum | solution.py:215
  (22 shorter events, 3.2 us)
Async XLA Ops:
  6.5 1.5 copy-start
  24.9 26.1 %copy-start.2 = (s32[64,64]{1,0:T(8,128)S(1)}, s32[64,64]{1,0:T(8,128)}, u32[]{:S(2)}) copy-start(s32[64,64]{1,0:T(8,128)} %param.13) | copy-start | bytes 49156
  24.9 20.6 %all-to-all-start = ((bf16[4,1032,128]{2,1,0:T(8,128)(2,1)}), bf16[4,1032,128]{2,1,0:T(8,128)(2,1)S(1)}, u32[]{:S(2)}, u32[]{:S(2)}) async-start(bf16[4,1032,128]{2,1,0:T(8,128)(2,1)} %pad_maximum_fusion), calls=%async_computation | async-start | bytes 2113536 | tf_op jit(solution)/shard_map/all_to_all | solution.py:184
  29.5 44.0 %all-gather.5.cloned.1.call-start = ((), (), s32[]{:S(2)}) async-start(), calls=%async_computation.4 | async-start | bytes 1320960 | tf_op jit(solution)/shard_map/all_gather | solution.py:201
  46.3 63.9 %all-gather.7.cloned.1.call-start = ((), (), s32[]{:S(2)}) async-start(), calls=%async_computation.5 | async-start | bytes 3962880 | tf_op jit(solution)/shard_map/all_gather | solution.py:201
  47.4 13.8 %all-to-all-start.1 = ((bf16[4,512,128]{2,1,0:T(8,128)(2,1)}), bf16[4,512,128]{2,1,0:T(8,128)(2,1)S(1)}, u32[]{:S(2)}, u32[]{:S(2)}) async-start(bf16[4,512,128]{2,1,0:T(8,128)(2,1)} %slice_bitcast_fusion), calls=%async_computation.1 | async-start | bytes 1048576 | tf_op jit(solution)/shard_map/all_to_all | solution.py:186
  61.1 0.8 copy-start.1
Sparse Core Ops, SparseCore 0:
  46.4 22.6 all-gather.4
  70.8 39.4 all-gather.6

commit v4 on v3

--- a/solution.py
+++ b/solution.py
@@ -206,9 +206,9 @@
         carry = attend_remote(own, qvis, queries, kv_all, key_hot, carry, score_scale, i == len(bounds) - 1)
     attended = carry
     back = lax.all_to_all(attended.reshape(heads_here, tok, lane), "yc", 0, 0, tiled=True)
-    mixed = jnp.einsum(
-        "hrd,hdo->ro", back, out_weight, preferred_element_type=jnp.float32
-    ).astype(jnp.bfloat16)
+    rows_all = jnp.transpose(back, (1, 0, 2)).reshape(tok, heads_here * head_size)
+    ow = out_weight.reshape(heads_here * head_size, out_weight.shape[2])
+    mixed = jnp.dot(rows_all, ow, preferred_element_type=jnp.float32).astype(jnp.bfloat16)
     groups = lax.axis_size("head")
     parts = mixed.reshape(groups, mixed.shape[0] // groups, mixed.shape[1])
     parts = lax.all_to_all(parts, "head", 0, 0)

time: 234 us -> 234 us (level)
  no operation moved by 1% of the time
where the time goes in v4:
time: 234 us; the launch traced here: 232 us
  blocking collectives  68.2 us (29%)
  waiting for transfers between devices  57.1 us (24%)
  Pallas kernels  47.4 us (20%)
  matrix products  21.9 us (9%)
  between operations  13.5 us (6%)
  other arithmetic  10.5 us (4%)
  starting transfers between devices  8.3 us (4%)
  local copies, waits for them, and re-layouts  4.63 us (2%)
    all_to_all x1, blocking collectives, per_device_body(): parts = lax.all_to_all(parts, 'head', 0, 0)  53.5 us
    pallas_call x2, Pallas kernels, attend_remote(): pl.pallas_call(kernel, grid_spec=grid_spec, out_shape=out_shape, compiler...  35.8 us
    all_gather x2, waiting for transfers between devices, per_device_body(): gathered.append(lax.all_gather(exch[lo:hi], 'x', axis=0))  35.2 us
    all_to_all x1, waiting for transfers between devices, per_device_body(): exch = lax.all_to_all(kv_part, 'yc', 0, 0, tiled=True)  15.2 us
    all_to_all x1, blocking collectives, per_device_body(): lax.all_to_all(attended.reshape(heads_here, tok, lane), 'yc', 0, 0, tiled...  14.7 us
    pallas_call x1, Pallas kernels, attend_local(): pl.pallas_call(functools.partial(local_kernel, scale=scale), grid=(nsteps...  11.6 us
    dot_general x1, matrix products, per_device_body(): jnp.einsum('td,dchk->hctk', moduled, qkv_weight, preferred_element_type=j...  10 us
    all_to_all x1, waiting for transfers between devices, per_device_body(): exch_q = lax.all_to_all(q_part, 'yc', 0, 0, tiled=True)  6.64 us
  transfers between devices with their start and end apart: 4, of which 3 were waited for; matrix products, arithmetic and copies ran while one was open for 3% of the time, Pallas kernels for 5%

profile of v4, /device:TPU:6, one launch (start us, length us, event | category | flops | bytes accessed | tf_op | source)
XLA Modules:
  0.0 231.5 jit_solution(5510216117090102585)
XLA Ops:
  7.3 0.8 select_reduce_fusion
  8.1 5.6 %fusion.2 = bf16[512,4096,1,1]{1,0,3,2:T(8,128)(2,1)S(1)} fusion(f32[16,4096]{1,0:T(8,128)S(1)} %copy-done, bf16[512,4096]{1,0:T(8,128)(2,1)} %param.7, s32[512]{0:T(512)S(1)} %select_reduce_fusion), kind=kOutput, calls=%fused_computation.4 | convolution fusion | flops 411049984 | bytes 8652800 | tf_op jit(solution)/shard_map/dot_general | solution.py:169
  13.7 10.0 %fusion.7 = bf16[4,3,512,128]{3,2,0,1:T(8,128)(2,1)S(1)} fusion(bf16[512,4096,1,1]{1,0,3,2:T(8,128)(2,1)S(1)} %fusion.2, bf16[4096,3,4,128]{3,2,1,0:T(4,128)(2,1)} %param.8), kind=kOutput, calls=%fused_computation.9 | convolution fusion | flops 6443237376 | bytes 18350080 | tf_op jit(solution)/shard_map/td,dchk->hctk/dot_general | solution.py:171
  23.9 1.0 pad_maximum_fusion
  24.9 4.6 %all-to-all-start = ((bf16[4,1032,128]{2,1,0:T(8,128)(2,1)}), bf16[4,1032,128]{2,1,0:T(8,128)(2,1)S(1)}, u32[]{:S(2)}, u32[]{:S(2)}) async-start(bf16[4,1032,128]{2,1,0:T(8,128)(2,1)} %pad_maximum_fusion), calls=%async_computation | async-start | bytes 2113536 | tf_op jit(solution)/shard_map/all_to_all | solution.py:184
  29.5 0.8 slice_bitcast_fusion
  30.4 15.2 %all-to-all-done = bf16[4,1032,128]{2,1,0:T(8,128)(2,1)S(1)} async-done(((bf16[4,1032,128]{2,1,0:T(8,128)(2,1)}), bf16[4,1032,128]{2,1,0:T(8,128)(2,1)S(1)}, u32[]{:S(2)}, u32[]{:S(2)}) %all-to-all-start) | async-done | bytes 1056800 | tf_op jit(solution)/shard_map/all_to_all | solution.py:184
  46.4 0.9 slice.32
  47.4 3.7 %all-to-all-start.1 = ((bf16[4,512,128]{2,1,0:T(8,128)(2,1)}), bf16[4,512,128]{2,1,0:T(8,128)(2,1)S(1)}, u32[]{:S(2)}, u32[]{:S(2)}) async-start(bf16[4,512,128]{2,1,0:T(8,128)(2,1)} %slice_bitcast_fusion), calls=%async_computation.1 | async-start | bytes 1048576 | tf_op jit(solution)/shard_map/all_to_all | solution.py:186
  51.0 1.5 convolution_convert_fusion.qvis_ref
  52.6 1.2 fusion.16
  53.7 0.8 fusion.13.kh_ref
  54.5 6.6 %all-to-all-done.1 = bf16[4,512,128]{2,1,0:T(8,128)(2,1)S(1)} async-done(((bf16[4,512,128]{2,1,0:T(8,128)(2,1)}), bf16[4,512,128]{2,1,0:T(8,128)(2,1)S(1)}, u32[]{:S(2)}, u32[]{:S(2)}) %all-to-all-start.1) | async-done | bytes 524320 | tf_op jit(solution)/shard_map/all_to_all | solution.py:186
  61.1 0.8 copy-done.1
  61.9 11.6 %shard_map.73 = (f32[2048,128]{1,0:T(8,128)}, f32[2048,128]{1,0:T(8,128)}, f32[2048,128]{1,0:T(8,128)}) custom-call(bf16[2048,64]{1,0:T(8,128)(2,1)} %convolution_convert_fusion.qvis_ref, bf16[2048,128]{1,0:T(8,128)(2,1)} %bitcast.37, bf16[2048,128]{1,0:T(8,128)(2,1)} %bitcast.42, bf16[2048,128]{1,0:T(8,128)(2,1)} %bitcast.41, bf16[64,2048]{1,0:T(8,128)(2,1)} %fusion.13.kh_ref), custom_call_target="tpu_custom_call" | custom-call | flops 2684354560 | bytes 4194304 | tf_op jit(solution)/shard_map/pallas_call | solution.py:77
  74.3 0.8 fusion.12.kh_ref
  75.0 35.2 %all-gather.7.cloned.1.call-done = bf16[12,1032,128]{2,1,0:T(8,128)(2,1)} async-done(((bf16[3,1032,128]{2,1,0:T(8,128)(2,1)}), bf16[12,1032,128]{2,1,0:T(8,128)(2,1)}) %all-gather.7.cloned.1.call-update) | async-done | bytes 3170320 | tf_op jit(solution)/shard_map/all_gather | solution.py:201
  111.0 1.1 fusion.6.kh_ref
  112.2 25.1 %shard_map.74 = (f32[2048,128]{1,0:T(8,128)}, f32[2048,128]{1,0:T(8,128)}, f32[2048,128]{1,0:T(8,128)}) custom-call(s32[1]{0:T(128)} %bitcast.own_ref, bf16[2048,64]{1,0:T(8,128)(2,1)} %convolution_convert_fusion.qvis_ref, bf16[2048,128]{1,0:T(8,128)(2,1)} %bitcast.38, bf16[4,3,1032,128]{3,2,1,0:T(8,128)(2,1)} %bitcast.46, ...), custom_call_target="tpu_custom_call" | custom-call | flops 6039797760 | bytes 5505024 | tf_op jit(solution)/shard_map/pallas_call | solution.py:145
  137.3 10.6 %shard_map.75 = bf16[2048,128]{1,0:T(8,128)(2,1)} custom-call(s32[1]{0:T(128)} %bitcast.own_ref, bf16[2048,64]{1,0:T(8,128)(2,1)} %convolution_convert_fusion.qvis_ref, bf16[2048,128]{1,0:T(8,128)(2,1)} %bitcast.39, bf16[4,1,1032,128]{3,2,1,0:T(8,128)(2,1)} %bitcast.49, bf16[4,1,1032,128]{3,2,1,0:T(8,128)(2,1)} %bitcast.50, ...), custom_call_target="tpu_custom_call" | custom-call | flops 2013265920 | bytes 3932160 | tf_op jit(solution)/shard_map/pallas_call | solution.py:145
  147.9 14.7 %all_to_all.20 = bf16[4,512,128]{2,1,0:T(8,128)(2,1)S(1)} all-to-all(bf16[4,512,128]{2,1,0:T(8,128)(2,1)} %bitcast.40), channel_id=1, replica_groups=mesh['x'=4,'yc'=4,'head'=8] {'yc'}, dimensions={0} | all-to-all | bytes 1048576 | tf_op jit(solution)/shard_map/all_to_all | solution.py:208
  162.6 4.7 %bitcast_convert_fusion = bf16[512,4096]{1,0:T(8,128)(2,1)S(1)} fusion(bf16[4,128,4096]{2,1,0:T(8,128)(2,1)} %param.9, bf16[4,512,128]{2,1,0:T(8,128)(2,1)S(1)} %all_to_all.20), kind=kOutput, calls=%fused_computation.2 | convolution fusion | flops 2149580800 | bytes 8912896 | tf_op jit(solution)/shard_map/dot_general | solution.py:211
  167.4 53.5 %all_to_all.21 = bf16[8,64,4096]{2,1,0:T(8,128)(2,1)} all-to-all(bf16[8,64,4096]{2,1,0:T(8,128)(2,1)S(1)} %bitcast.35), channel_id=1, replica_groups=mesh['x'=4,'yc'=4,'head'=8] {'head'}, dimensions={0} | all-to-all | bytes 8388608 | tf_op jit(solution)/shard_map/all_to_all | solution.py:214
  220.8 3.8 %reduce_sum.22 = bf16[64,4096]{1,0:T(8,128)(2,1)} reduce(bf16[8,64,4096]{2,1,0:T(8,128)(2,1)} %all_to_all.21, bf16[]{:T(256)} %constant.13.clone.1), dimensions={0}, to_apply=%region_1.2 | reduce | flops 1835008 | bytes 4718594 | tf_op jit(solution)/shard_map/reduce_sum | solution.py:215
  (22 shorter events, 3.2 us)
Async XLA Ops:
  6.5 1.5 copy-start
  24.9 26.1 %copy-start.2 = (s32[64,64]{1,0:T(8,128)S(1)}, s32[64,64]{1,0:T(8,128)}, u32[]{:S(2)}) copy-start(s32[64,64]{1,0:T(8,128)} %param.13) | copy-start | bytes 49156
  24.9 20.6 %all-to-all-start = ((bf16[4,1032,128]{2,1,0:T(8,128)(2,1)}), bf16[4,1032,128]{2,1,0:T(8,128)(2,1)S(1)}, u32[]{:S(2)}, u32[]{:S(2)}) async-start(bf16[4,1032,128]{2,1,0:T(8,128)(2,1)} %pad_maximum_fusion), calls=%async_computation | async-start | bytes 2113536 | tf_op jit(solution)/shard_map/all_to_all | solution.py:184
  29.5 44.0 %all-gather.5.cloned.1.call-start = ((), (), s32[]{:S(2)}) async-start(), calls=%async_computation.4 | async-start | bytes 1320960 | tf_op jit(solution)/shard_map/all_gather | solution.py:201
  46.3 63.9 %all-gather.7.cloned.1.call-start = ((), (), s32[]{:S(2)}) async-start(), calls=%async_computation.5 | async-start | bytes 3962880 | tf_op jit(solution)/shard_map/all_gather | solution.py:201
  47.4 13.8 %all-to-all-start.1 = ((bf16[4,512,128]{2,1,0:T(8,128)(2,1)}), bf16[4,512,128]{2,1,0:T(8,128)(2,1)S(1)}, u32[]{:S(2)}, u32[]{:S(2)}) async-start(bf16[4,512,128]{2,1,0:T(8,128)(2,1)} %slice_bitcast_fusion), calls=%async_computation.1 | async-start | bytes 1048576 | tf_op jit(solution)/shard_map/all_to_all | solution.py:186
  61.1 0.8 copy-start.1
Sparse Core Ops, SparseCore 0:
  46.4 22.6 all-gather.4
  70.8 39.4 all-gather.6

commit v5 on v4

--- a/solution.py
+++ b/solution.py
@@ -168,8 +168,8 @@
     level_hot = (level_rows[:, None] == level_ids).astype(jnp.float32)
     modulation = jnp.dot(level_hot, mod_table, precision=lax.Precision.HIGHEST)
     moduled = (activations.astype(jnp.float32) * (1.0 + modulation)).astype(jnp.bfloat16)
-    qkv = jnp.einsum(
-        "td,dchk->hctk", moduled, qkv_weight, preferred_element_type=jnp.float32
+    kv_proj = jnp.einsum(
+        "td,dchk->hctk", moduled, qkv_weight[:, 1:3], preferred_element_type=jnp.float32
     ).astype(jnp.bfloat16)
     lane = head_size
     clip_rows = tok // lane
@@ -178,11 +178,14 @@
         [clip_of.astype(jnp.bfloat16).reshape(clip_rows, lane), jnp.zeros((pad_rows, lane), jnp.bfloat16)]
     )
     kv_part = jnp.concatenate(
-        [qkv[:, 1:3].reshape(heads_here, 2 * tok, lane), jnp.broadcast_to(clip_slab, (heads_here,) + clip_slab.shape)],
+        [kv_proj.reshape(heads_here, 2 * tok, lane), jnp.broadcast_to(clip_slab, (heads_here,) + clip_slab.shape)],
         axis=1,
     )
     exch = lax.all_to_all(kv_part, "yc", 0, 0, tiled=True)
-    q_part, exch = lax.optimization_barrier((qkv[:, 0], exch))
+    q_proj = jnp.einsum(
+        "td,dhk->htk", moduled, qkv_weight[:, 0], preferred_element_type=jnp.float32
+    ).astype(jnp.bfloat16)
+    q_part, exch = lax.optimization_barrier((q_proj, exch))
     exch_q = lax.all_to_all(q_part, "yc", 0, 0, tiled=True)
     group_tok = heads_here * tok
     queries = exch_q.reshape(group_tok, lane)

time: 234 us -> 229 us (0.979)
  waiting for transfers between devices: 57.1 us -> 51.3 us
  local copies, waits for them, and re-layouts: 4.63 us -> 9.37 us
  matrix products: 21.9 us -> 18 us
    all_to_all x1, waiting for transfers between devices: 15.2 us -> 9.39 us  [per_device_body(): exch = lax.all_to_all(kv_part, 'yc', 0, 0, tiled=True)]
    unnamed x7 -> x15, local copies, waits for them, and re-layouts: 0.8 us -> 4.25 us
    dot_general x1 -> x2, matrix products: 10 us -> 7.65 us  [the longest x1 4.49 us: per_device_body(): jnp.einsum('td,dchk->hctk', moduled, qkv_weight[:, 1:3], preferred_elemen...]
  transfers between devices with their start and end apart: 4 -> 4, of which waited for: 3 -> 3; matrix products, arithmetic and copies ran while one was open for 3% -> 4% of each run, Pallas kernels for 5% -> 5%
where the time goes in v5:
time: 229 us; the launch traced here: 227 us
  blocking collectives  68.3 us (30%)
  waiting for transfers between devices  51.3 us (22%)
  Pallas kernels  47.4 us (21%)
  matrix products  18 us (8%)
  between operations  13.5 us (6%)
  other arithmetic  10.5 us (5%)
  local copies, waits for them, and re-layouts  9.37 us (4%)
  starting transfers between devices  8.17 us (4%)
    all_to_all x1, blocking collectives, per_device_body(): parts = lax.all_to_all(parts, 'head', 0, 0)  53.6 us
    pallas_call x2, Pallas kernels, attend_remote(): pl.pallas_call(kernel, grid_spec=grid_spec, out_shape=out_shape, compiler...  35.8 us
    all_gather x2, waiting for transfers between devices, per_device_body(): gathered.append(lax.all_gather(exch[lo:hi], 'x', axis=0))  35.2 us
    all_to_all x1, blocking collectives, per_device_body(): lax.all_to_all(attended.reshape(heads_here, tok, lane), 'yc', 0, 0, tiled...  14.7 us
    pallas_call x1, Pallas kernels, attend_local(): pl.pallas_call(functools.partial(local_kernel, scale=scale), grid=(nsteps...  11.6 us
    all_to_all x1, waiting for transfers between devices, per_device_body(): exch = lax.all_to_all(kv_part, 'yc', 0, 0, tiled=True)  9.39 us
    all_to_all x1, waiting for transfers between devices, per_device_body(): exch_q = lax.all_to_all(q_part, 'yc', 0, 0, tiled=True)  6.68 us
    dot_general x1, matrix products, per_device_body(): jnp.dot(rows_all, ow, preferred_element_type=jnp.float32)  4.73 us
  transfers between devices with their start and end apart: 4, of which 3 were waited for; matrix products, arithmetic and copies ran while one was open for 4% of the time, Pallas kernels for 5%

profile of v5, /device:TPU:6, one launch (start us, length us, event | category | flops | bytes accessed | tf_op | source)
XLA Modules:
  0.0 226.6 jit_solution(10301765391752151228)
XLA Ops:
  7.3 0.8 select_reduce_fusion
  8.1 2.2 copy-done.2
  10.2 4.1 %multiply_convert_fusion = bf16[512,4096]{1,0:T(8,128)(2,1)S(1)} fusion(bf16[512,4096]{1,0:T(8,128)(2,1)S(1)} %copy-done.2, f32[16,4096]{1,0:T(8,128)S(1)} %copy-done, s32[512]{0:T(512)S(1)} %select_reduce_fusion), kind=kOutput, calls=%fused_computation.3 | convolution fusion | flops 411049984 | bytes 8652800 | tf_op jit(solution)/shard_map/dot_general | solution.py:169
  14.4 4.5 %fusion.11 = bf16[4,2,512,128]{3,2,0,1:T(8,128)(2,1)S(1)} fusion(bf16[4096,2,4,128]{3,2,1,0:T(4,128)(2,1)S(1)} %slice-done, bf16[512,4096]{1,0:T(8,128)(2,1)S(1)} %multiply_convert_fusion), kind=kOutput, calls=%fused_computation.12 | convolution fusion | flops 4295491584 | bytes 13631488 | tf_op jit(solution)/shard_map/td,dchk->hctk/dot_general | solution.py:171
  19.0 1.0 pad_maximum_fusion
  20.0 4.5 %all-to-all-start = ((bf16[4,1032,128]{2,1,0:T(8,128)(2,1)}), bf16[4,1032,128]{2,1,0:T(8,128)(2,1)S(1)}, u32[]{:S(2)}, u32[]{:S(2)}) async-start(bf16[4,1032,128]{2,1,0:T(8,128)(2,1)} %pad_maximum_fusion), calls=%async_computation | async-start | bytes 2113536 | tf_op jit(solution)/shard_map/all_to_all | solution.py:184
  24.5 2.2 slice-done.1
  26.7 1.3 copy-done.4
  28.0 3.2 %fusion.19 = bf16[4,512,128]{2,1,0:T(8,128)(2,1)} fusion(bf16[4096,1,4,128]{3,2,1,0:T(4,128)(2,1)S(1)} %slice-done.1, bf16[512,4096]{1,0:T(8,128)(2,1)S(1)} %copy-done.4), kind=kOutput, calls=%fused_computation.14 | convolution fusion | flops 2147745792 | bytes 8912896 | tf_op jit(solution)/shard_map/td,dhk->htk/dot_general | solution.py:185
  31.1 9.4 %all-to-all-done = bf16[4,1032,128]{2,1,0:T(8,128)(2,1)S(1)} async-done(((bf16[4,1032,128]{2,1,0:T(8,128)(2,1)}), bf16[4,1032,128]{2,1,0:T(8,128)(2,1)S(1)}, u32[]{:S(2)}, u32[]{:S(2)}) %all-to-all-start) | async-done | bytes 1056800 | tf_op jit(solution)/shard_map/all_to_all | solution.py:184
  41.3 1.0 slice.32
  42.4 3.7 %all-to-all-start.1 = ((bf16[4,512,128]{2,1,0:T(8,128)(2,1)}), bf16[4,512,128]{2,1,0:T(8,128)(2,1)S(1)}, u32[]{:S(2)}, u32[]{:S(2)}) async-start(bf16[4,512,128]{2,1,0:T(8,128)(2,1)} %fusion.19), calls=%async_computation.1 | async-start | bytes 1048576 | tf_op jit(solution)/shard_map/all_to_all | solution.py:189
  46.0 1.5 convolution_convert_fusion.qvis_ref
  47.6 1.1 fusion.28
  49.4 6.7 %all-to-all-done.1 = bf16[4,512,128]{2,1,0:T(8,128)(2,1)S(1)} async-done(((bf16[4,512,128]{2,1,0:T(8,128)(2,1)}), bf16[4,512,128]{2,1,0:T(8,128)(2,1)S(1)}, u32[]{:S(2)}, u32[]{:S(2)}) %all-to-all-start.1) | async-done | bytes 524320 | tf_op jit(solution)/shard_map/all_to_all | solution.py:189
  56.9 11.6 %shard_map.73 = (f32[2048,128]{1,0:T(8,128)}, f32[2048,128]{1,0:T(8,128)}, f32[2048,128]{1,0:T(8,128)}) custom-call(bf16[2048,64]{1,0:T(8,128)(2,1)} %convolution_convert_fusion.qvis_ref, bf16[2048,128]{1,0:T(8,128)(2,1)} %bitcast.55, bf16[2048,128]{1,0:T(8,128)(2,1)} %bitcast.60, bf16[2048,128]{1,0:T(8,128)(2,1)} %bitcast.59, bf16[64,2048]{1,0:T(8,128)(2,1)} %fusion.25.kh_ref), custom_call_target="tpu_custom_call" | custom-call | flops 2684354560 | bytes 4194304 | tf_op jit(solution)/shard_map/pallas_call | solution.py:77
  70.0 35.2 %all-gather.7.cloned.1.call-done = bf16[12,1032,128]{2,1,0:T(8,128)(2,1)} async-done(((bf16[3,1032,128]{2,1,0:T(8,128)(2,1)}), bf16[12,1032,128]{2,1,0:T(8,128)(2,1)}) %all-gather.7.cloned.1.call-update) | async-done | bytes 3170320 | tf_op jit(solution)/shard_map/all_gather | solution.py:204
  106.0 1.1 fusion.5.kh_ref
  107.1 25.2 %shard_map.74 = (f32[2048,128]{1,0:T(8,128)}, f32[2048,128]{1,0:T(8,128)}, f32[2048,128]{1,0:T(8,128)}) custom-call(s32[1]{0:T(128)} %bitcast.own_ref, bf16[2048,64]{1,0:T(8,128)(2,1)} %convolution_convert_fusion.qvis_ref, bf16[2048,128]{1,0:T(8,128)(2,1)} %bitcast.56, bf16[4,3,1032,128]{3,2,1,0:T(8,128)(2,1)} %bitcast.64, ...), custom_call_target="tpu_custom_call" | custom-call | flops 6039797760 | bytes 5505024 | tf_op jit(solution)/shard_map/pallas_call | solution.py:145
  132.2 10.6 %shard_map.75 = bf16[2048,128]{1,0:T(8,128)(2,1)} custom-call(s32[1]{0:T(128)} %bitcast.own_ref, bf16[2048,64]{1,0:T(8,128)(2,1)} %convolution_convert_fusion.qvis_ref, bf16[2048,128]{1,0:T(8,128)(2,1)} %bitcast.57, bf16[4,1,1032,128]{3,2,1,0:T(8,128)(2,1)} %bitcast.67, bf16[4,1,1032,128]{3,2,1,0:T(8,128)(2,1)} %bitcast.68, ...), custom_call_target="tpu_custom_call" | custom-call | flops 2013265920 | bytes 3932160 | tf_op jit(solution)/shard_map/pallas_call | solution.py:145
  142.9 14.7 %all_to_all.20 = bf16[4,512,128]{2,1,0:T(8,128)(2,1)S(1)} all-to-all(bf16[4,512,128]{2,1,0:T(8,128)(2,1)} %bitcast.58), channel_id=1, replica_groups=mesh['x'=4,'yc'=4,'head'=8] {'yc'}, dimensions={0} | all-to-all | bytes 1048576 | tf_op jit(solution)/shard_map/all_to_all | solution.py:211
  157.6 4.7 %bitcast_convert_fusion = bf16[512,4096]{1,0:T(8,128)(2,1)S(1)} fusion(bf16[4,128,4096]{2,1,0:T(8,128)(2,1)} %param.9, bf16[4,512,128]{2,1,0:T(8,128)(2,1)S(1)} %all_to_all.20), kind=kOutput, calls=%fused_computation.2 | convolution fusion | flops 2149580800 | bytes 8912896 | tf_op jit(solution)/shard_map/dot_general | solution.py:214
  162.4 53.6 %all_to_all.21 = bf16[8,64,4096]{2,1,0:T(8,128)(2,1)} all-to-all(bf16[8,64,4096]{2,1,0:T(8,128)(2,1)S(1)} %bitcast.53), channel_id=1, replica_groups=mesh['x'=4,'yc'=4,'head'=8] {'head'}, dimensions={0} | all-to-all | bytes 8388608 | tf_op jit(solution)/shard_map/all_to_all | solution.py:217
  215.9 3.8 %reduce_sum.22 = bf16[64,4096]{1,0:T(8,128)(2,1)} reduce(bf16[8,64,4096]{2,1,0:T(8,128)(2,1)} %all_to_all.21, bf16[]{:T(256)} %constant.13.clone.1), dimensions={0}, to_apply=%region_1.2 | reduce | flops 1835008 | bytes 4718594 | tf_op jit(solution)/shard_map/reduce_sum | solution.py:218
  (33 shorter events, 5.4 us)
Async XLA Ops:
  6.5 1.5 copy-start
  8.1 2.2 copy-start.2
  10.2 4.1 %slice-start = ((bf16[4096,3,4,128]{3,2,1,0:T(4,128)(2,1)}), bf16[4096,2,4,128]{3,2,1,0:T(4,128)(2,1)S(1)}, s32[]{:S(2)}) async-start(bf16[4096,3,4,128]{3,2,1,0:T(4,128)(2,1)} %param.8), calls=%async_computation.6 | async-start | bytes 16777216 | tf_op jit(solution)/shard_map/slice | solution.py:172
  14.4 4.5 %copy-start.3 = (bf16[512,4096]{1,0:T(8,128)(2,1)}, bf16[512,4096]{1,0:T(8,128)(2,1)S(1)}, u32[]{:S(2)}) copy-start(bf16[512,4096]{1,0:T(8,128)(2,1)S(1)} %multiply_convert_fusion) | copy-start | bytes 12582916
  20.0 20.5 %all-to-all-start = ((bf16[4,1032,128]{2,1,0:T(8,128)(2,1)}), bf16[4,1032,128]{2,1,0:T(8,128)(2,1)S(1)}, u32[]{:S(2)}, u32[]{:S(2)}) async-start(bf16[4,1032,128]{2,1,0:T(8,128)(2,1)} %pad_maximum_fusion), calls=%async_computation | async-start | bytes 2113536 | tf_op jit(solution)/shard_map/all_to_all | solution.py:184
  24.5 44.0 %all-gather.5.cloned.1.call-start = ((), (), s32[]{:S(2)}) async-start(), calls=%async_computation.4 | async-start | bytes 1320960 | tf_op jit(solution)/shard_map/all_gather | solution.py:204
  24.5 2.2 slice-start.1
  24.5 3.5 %copy-start.4 = (bf16[512,4096]{1,0:T(8,128)(2,1)S(1)}, bf16[512,4096]{1,0:T(8,128)(2,1)}, u32[]{:S(2)}) copy-start(bf16[512,4096]{1,0:T(8,128)(2,1)} %copy-done.3) | copy-start | bytes 12582916
  31.1 14.9 %copy-start.6 = (s32[64,64]{1,0:T(8,128)S(1)}, s32[64,64]{1,0:T(8,128)}, u32[]{:S(2)}) copy-start(s32[64,64]{1,0:T(8,128)} %param.13) | copy-start | bytes 49156
  41.3 63.9 %all-gather.7.cloned.1.call-start = ((), (), s32[]{:S(2)}) async-start(), calls=%async_computation.5 | async-start | bytes 3962880 | tf_op jit(solution)/shard_map/all_gather | solution.py:204
  42.4 13.8 %all-to-all-start.1 = ((bf16[4,512,128]{2,1,0:T(8,128)(2,1)}), bf16[4,512,128]{2,1,0:T(8,128)(2,1)S(1)}, u32[]{:S(2)}, u32[]{:S(2)}) async-start(bf16[4,512,128]{2,1,0:T(8,128)(2,1)} %fusion.19), calls=%async_computation.1 | async-start | bytes 1048576 | tf_op jit(solution)/shard_map/all_to_all | solution.py:189
  56.1 0.8 copy-start.5
  162.3 57.4 %copy-start.1 = (f32[16,4096]{1,0:T(8,128)S(1)}, f32[16,4096]{1,0:T(8,128)}, u32[]{:S(2)}) copy-start(f32[16,4096]{1,0:T(8,128)} %param.10) | copy-start | bytes 786436
Sparse Core Ops, SparseCore 0:
  41.4 22.6 all-gather.4
  65.7 39.4 all-gather.6

commit v6 on v5

--- a/solution.py
+++ b/solution.py
@@ -211,11 +211,17 @@
     back = lax.all_to_all(attended.reshape(heads_here, tok, lane), "yc", 0, 0, tiled=True)
     rows_all = jnp.transpose(back, (1, 0, 2)).reshape(tok, heads_here * head_size)
     ow = out_weight.reshape(heads_here * head_size, out_weight.shape[2])
-    mixed = jnp.dot(rows_all, ow, preferred_element_type=jnp.float32).astype(jnp.bfloat16)
     groups = lax.axis_size("head")
-    parts = mixed.reshape(groups, mixed.shape[0] // groups, mixed.shape[1])
-    parts = lax.all_to_all(parts, "head", 0, 0)
-    return jnp.sum(parts.astype(jnp.float32), axis=0).astype(jnp.bfloat16)
+    width = ow.shape[1] // 2
+    outs = []
+    for c in range(2):
+        mixed = jnp.dot(
+            rows_all, ow[:, c * width:(c + 1) * width], preferred_element_type=jnp.float32
+        ).astype(jnp.bfloat16)
+        parts = mixed.reshape(groups, mixed.shape[0] // groups, width)
+        parts = lax.all_to_all(parts, "head", 0, 0)
+        outs.append(jnp.sum(parts.astype(jnp.float32), axis=0).astype(jnp.bfloat16))
+    return jnp.concatenate(outs, axis=1)
 
 
 def solution(mesh):

time: 229 us -> 237 us (1.035)
  blocking collectives: 68.3 us -> 14.6 us
  waiting for transfers between devices: 51.3 us -> 99.2 us
  starting transfers between devices: 8.17 us -> 17.1 us
  matrix products: 18 us -> 21.7 us
    all_to_all x1 -> x0, blocking collectives: 53.6 us -> none  [per_device_body(): parts = lax.all_to_all(parts, 'head', 0, 0)]
    all_to_all x0 -> x2, waiting for transfers between devices: none -> 47.8 us  [per_device_body(): parts = lax.all_to_all(parts, 'head', 0, 0)]
    all_to_all x0 -> x2, starting transfers between devices: none -> 8.93 us  [per_device_body(): parts = lax.all_to_all(parts, 'head', 0, 0)]
    dot_general x1 -> x2, matrix products: 4.73 us -> 8.39 us  [per_device_body(): jnp.dot(rows_all, ow[:, c * width:(c + 1) * width], preferred_element_typ...]
  transfers between devices with their start and end apart: 4 -> 6, of which waited for: 3 -> 5; matrix products, arithmetic and copies ran while one was open for 4% -> 6% of each run, Pallas kernels for 5% -> 5%
where the time goes in v6:
time: 237 us; the launch traced here: 234 us
  waiting for transfers between devices  99.2 us (42%)
  Pallas kernels  47.4 us (20%)
  matrix products  21.7 us (9%)
  starting transfers between devices  17.1 us (7%)
  blocking collectives  14.6 us (6%)
  between operations  13.6 us (6%)
  local copies, waits for them, and re-layouts  10.6 us (4%)
  other arithmetic  9.8 us (4%)
    all_to_all x2, waiting for transfers between devices, per_device_body(): parts = lax.all_to_all(parts, 'head', 0, 0)  47.8 us
    pallas_call x2, Pallas kernels, attend_remote(): pl.pallas_call(kernel, grid_spec=grid_spec, out_shape=out_shape, compiler...  35.8 us
    all_gather x2, waiting for transfers between devices, per_device_body(): gathered.append(lax.all_gather(exch[lo:hi], 'x', axis=0))  35.3 us
    all_to_all x1, blocking collectives, per_device_body(): lax.all_to_all(attended.reshape(heads_here, tok, lane), 'yc', 0, 0, tiled...  14.6 us
    pallas_call x1, Pallas kernels, attend_local(): pl.pallas_call(functools.partial(local_kernel, scale=scale), grid=(nsteps...  11.6 us
    all_to_all x1, waiting for transfers between devices, per_device_body(): exch = lax.all_to_all(kv_part, 'yc', 0, 0, tiled=True)  9.41 us
    all_to_all x2, starting transfers between devices, per_device_body(): parts = lax.all_to_all(parts, 'head', 0, 0)  8.93 us
    dot_general x2, matrix products, per_device_body(): jnp.dot(rows_all, ow[:, c * width:(c + 1) * width], preferred_element_typ...  8.39 us
  transfers between devices with their start and end apart: 6, of which 5 were waited for; matrix products, arithmetic and copies ran while one was open for 6% of the time, Pallas kernels for 5%

profile of v6, /device:TPU:6, one launch (start us, length us, event | category | flops | bytes accessed | tf_op | source)
XLA Modules:
  0.0 233.9 jit_solution(12048434289407143600)
XLA Ops:
  8.1 2.2 copy-done.2
  10.2 4.1 %multiply_convert_fusion = bf16[512,4096]{1,0:T(8,128)(2,1)S(1)} fusion(bf16[512,4096]{1,0:T(8,128)(2,1)S(1)} %copy-done.2, f32[16,4096]{1,0:T(8,128)S(1)} %copy-done, s32[512]{0:T(512)S(1)} %select_reduce_fusion), kind=kOutput, calls=%fused_computation.2 | convolution fusion | flops 411049984 | bytes 8652800 | tf_op jit(solution)/shard_map/dot_general | solution.py:169
  14.4 4.5 %fusion.13 = bf16[4,2,512,128]{3,2,0,1:T(8,128)(2,1)S(1)} fusion(bf16[4096,2,4,128]{3,2,1,0:T(4,128)(2,1)S(1)} %slice-done, bf16[512,4096]{1,0:T(8,128)(2,1)S(1)} %multiply_convert_fusion), kind=kOutput, calls=%fused_computation.15 | convolution fusion | flops 4295491584 | bytes 13631488 | tf_op jit(solution)/shard_map/td,dchk->hctk/dot_general | solution.py:171
  20.0 4.5 %all-to-all-start = ((bf16[4,1032,128]{2,1,0:T(8,128)(2,1)}), bf16[4,1032,128]{2,1,0:T(8,128)(2,1)S(1)}, u32[]{:S(2)}, u32[]{:S(2)}) async-start(bf16[4,1032,128]{2,1,0:T(8,128)(2,1)} %pad_maximum_fusion), calls=%async_computation | async-start | bytes 2113536 | tf_op jit(solution)/shard_map/all_to_all | solution.py:184
  24.5 2.2 slice-done.1
  26.7 1.3 copy-done.4
  28.0 3.1 %fusion.21 = bf16[4,512,128]{2,1,0:T(8,128)(2,1)} fusion(bf16[4096,1,4,128]{3,2,1,0:T(4,128)(2,1)S(1)} %slice-done.1, bf16[512,4096]{1,0:T(8,128)(2,1)S(1)} %copy-done.4), kind=kOutput, calls=%fused_computation.17 | convolution fusion | flops 2147745792 | bytes 8912896 | tf_op jit(solution)/shard_map/td,dhk->htk/dot_general | solution.py:185
  31.1 9.4 %all-to-all-done = bf16[4,1032,128]{2,1,0:T(8,128)(2,1)S(1)} async-done(((bf16[4,1032,128]{2,1,0:T(8,128)(2,1)}), bf16[4,1032,128]{2,1,0:T(8,128)(2,1)S(1)}, u32[]{:S(2)}, u32[]{:S(2)}) %all-to-all-start) | async-done | bytes 1056800 | tf_op jit(solution)/shard_map/all_to_all | solution.py:184
  42.3 3.7 %all-to-all-start.1 = ((bf16[4,512,128]{2,1,0:T(8,128)(2,1)}), bf16[4,512,128]{2,1,0:T(8,128)(2,1)S(1)}, u32[]{:S(2)}, u32[]{:S(2)}) async-start(bf16[4,512,128]{2,1,0:T(8,128)(2,1)} %fusion.21), calls=%async_computation.1 | async-start | bytes 1048576 | tf_op jit(solution)/shard_map/all_to_all | solution.py:189
  46.0 1.5 convolution_convert_fusion.2.qvis_ref
  49.4 6.7 %all-to-all-done.1 = bf16[4,512,128]{2,1,0:T(8,128)(2,1)S(1)} async-done(((bf16[4,512,128]{2,1,0:T(8,128)(2,1)}), bf16[4,512,128]{2,1,0:T(8,128)(2,1)S(1)}, u32[]{:S(2)}, u32[]{:S(2)}) %all-to-all-start.1) | async-done | bytes 524320 | tf_op jit(solution)/shard_map/all_to_all | solution.py:189
  56.9 11.6 %shard_map.73 = (f32[2048,128]{1,0:T(8,128)}, f32[2048,128]{1,0:T(8,128)}, f32[2048,128]{1,0:T(8,128)}) custom-call(bf16[2048,64]{1,0:T(8,128)(2,1)} %convolution_convert_fusion.2.qvis_ref, bf16[2048,128]{1,0:T(8,128)(2,1)} %bitcast.57, bf16[2048,128]{1,0:T(8,128)(2,1)} %bitcast.64, bf16[2048,128]{1,0:T(8,128)(2,1)} %bitcast.63, bf16[64,2048]{1,0:T(8,128)(2,1)} %fusion.26.kh_ref), custom_call_target="tpu_custom_call" | custom-call | flops 2684354560 | bytes 4194304 | tf_op jit(solution)/shard_map/pallas_call | solution.py:77
  70.0 35.3 %all-gather.7.cloned.1.call-done = bf16[12,1032,128]{2,1,0:T(8,128)(2,1)} async-done(((bf16[3,1032,128]{2,1,0:T(8,128)(2,1)}), bf16[12,1032,128]{2,1,0:T(8,128)(2,1)}) %all-gather.7.cloned.1.call-update) | async-done | bytes 3170320 | tf_op jit(solution)/shard_map/all_gather | solution.py:204
  107.1 25.1 %shard_map.74 = (f32[2048,128]{1,0:T(8,128)}, f32[2048,128]{1,0:T(8,128)}, f32[2048,128]{1,0:T(8,128)}) custom-call(s32[1]{0:T(128)} %bitcast.own_ref, bf16[2048,64]{1,0:T(8,128)(2,1)} %convolution_convert_fusion.2.qvis_ref, bf16[2048,128]{1,0:T(8,128)(2,1)} %bitcast.58, bf16[4,3,1032,128]{3,2,1,0:T(8,128)(2,1)} %bitcast.68, ...), custom_call_target="tpu_custom_call" | custom-call | flops 6039797760 | bytes 5505024 | tf_op jit(solution)/shard_map/pallas_call | solution.py:145
  132.3 10.6 %shard_map.75 = bf16[2048,128]{1,0:T(8,128)(2,1)} custom-call(s32[1]{0:T(128)} %bitcast.own_ref, bf16[2048,64]{1,0:T(8,128)(2,1)} %convolution_convert_fusion.2.qvis_ref, bf16[2048,128]{1,0:T(8,128)(2,1)} %bitcast.59, bf16[4,1,1032,128]{3,2,1,0:T(8,128)(2,1)} %bitcast.71, bf16[4,1,1032,128]{3,2,1,0:T(8,128)(2,1)} %bitcast.72, ...), custom_call_target="tpu_custom_call" | custom-call | flops 2013265920 | bytes 3932160 | tf_op jit(solution)/shard_map/pallas_call | solution.py:145
  142.9 1.2 copy.38
  144.2 14.6 %all_to_all.25 = bf16[4,512,128]{1,2,0:T(8,128)(2,1)S(1)} all-to-all(bf16[4,512,128]{1,2,0:T(8,128)(2,1)S(1)} %copy.38), channel_id=1, replica_groups=mesh['x'=4,'yc'=4,'head'=8] {'yc'}, dimensions={0} | all-to-all | bytes 1048576 | tf_op jit(solution)/shard_map/all_to_all | solution.py:211
  158.7 4.2 %convolution_convert_fusion.1 = bf16[512,2048]{1,0:T(8,128)(2,1)} fusion(bf16[512,512]{0,1:T(8,128)(2,1)S(1)} %bitcast.61, bf16[512,4096]{1,0:T(8,128)(2,1)} %bitcast.73), kind=kOutput, calls=%fused_computation.8 | convolution fusion | flops 1074790400 | bytes 4718592 | tf_op jit(solution)/shard_map/dot_general | solution.py:218
  162.9 4.5 %all-to-all-start.3 = ((bf16[8,64,2048]{2,1,0:T(8,128)(2,1)}), bf16[8,64,2048]{2,1,0:T(8,128)(2,1)S(1)}, u32[]{:S(2)}, u32[]{:S(2)}) async-start(bf16[8,64,2048]{2,1,0:T(8,128)(2,1)} %bitcast.56), calls=%async_computation.3 | async-start | bytes 4194304 | tf_op jit(solution)/shard_map/all_to_all | solution.py:222
  167.4 4.2 %convolution_convert_fusion = bf16[512,2048]{1,0:T(8,128)(2,1)} fusion(bf16[512,512]{0,1:T(8,128)(2,1)S(1)} %bitcast.62, bf16[512,4096]{1,0:T(8,128)(2,1)} %bitcast.74), kind=kOutput, calls=%fused_computation.7 | convolution fusion | flops 1074790400 | bytes 4718592 | tf_op jit(solution)/shard_map/dot_general | solution.py:218
  171.6 22.4 %all-to-all-done.3 = bf16[8,64,2048]{2,1,0:T(8,128)(2,1)S(1)} async-done(((bf16[8,64,2048]{2,1,0:T(8,128)(2,1)}), bf16[8,64,2048]{2,1,0:T(8,128)(2,1)S(1)}, u32[]{:S(2)}, u32[]{:S(2)}) %all-to-all-start.3) | async-done | bytes 2097184 | tf_op jit(solution)/shard_map/all_to_all | solution.py:222
  194.0 4.5 %all-to-all-start.4 = ((bf16[8,64,2048]{2,1,0:T(8,128)(2,1)}), bf16[8,64,2048]{2,1,0:T(8,128)(2,1)}, u32[]{:S(2)}, u32[]{:S(2)}) async-start(bf16[8,64,2048]{2,1,0:T(8,128)(2,1)} %bitcast.55), calls=%async_computation.4 | async-start | bytes 4194304 | tf_op jit(solution)/shard_map/all_to_all | solution.py:222
  198.8 25.4 %all-to-all-done.4 = bf16[8,64,2048]{2,1,0:T(8,128)(2,1)} async-done(((bf16[8,64,2048]{2,1,0:T(8,128)(2,1)}), bf16[8,64,2048]{2,1,0:T(8,128)(2,1)}, u32[]{:S(2)}, u32[]{:S(2)}) %all-to-all-start.4) | async-done | bytes 2097184 | tf_op jit(solution)/shard_map/all_to_all | solution.py:222
  224.2 2.0 reduce_sum.35
  (40 shorter events, 11.6 us)
Async XLA Ops:
  6.5 1.5 copy-start
  8.1 2.2 copy-start.2
  10.2 4.1 %slice-start = ((bf16[4096,3,4,128]{3,2,1,0:T(4,128)(2,1)}), bf16[4096,2,4,128]{3,2,1,0:T(4,128)(2,1)S(1)}, s32[]{:S(2)}) async-start(bf16[4096,3,4,128]{3,2,1,0:T(4,128)(2,1)} %param.8), calls=%async_computation.7 | async-start | bytes 16777216 | tf_op jit(solution)/shard_map/slice | solution.py:172
  14.4 4.5 %copy-start.3 = (bf16[512,4096]{1,0:T(8,128)(2,1)}, bf16[512,4096]{1,0:T(8,128)(2,1)S(1)}, u32[]{:S(2)}) copy-start(bf16[512,4096]{1,0:T(8,128)(2,1)S(1)} %multiply_convert_fusion) | copy-start | bytes 12582916
  20.0 20.5 %all-to-all-start = ((bf16[4,1032,128]{2,1,0:T(8,128)(2,1)}), bf16[4,1032,128]{2,1,0:T(8,128)(2,1)S(1)}, u32[]{:S(2)}, u32[]{:S(2)}) async-start(bf16[4,1032,128]{2,1,0:T(8,128)(2,1)} %pad_maximum_fusion), calls=%async_computation | async-start | bytes 2113536 | tf_op jit(solution)/shard_map/all_to_all | solution.py:184
  24.5 44.0 %all-gather.5.cloned.1.call-start = ((), (), s32[]{:S(2)}) async-start(), calls=%async_computation.5 | async-start | bytes 1320960 | tf_op jit(solution)/shard_map/all_gather | solution.py:204
  24.5 2.2 slice-start.1
  24.5 3.5 %copy-start.4 = (bf16[512,4096]{1,0:T(8,128)(2,1)S(1)}, bf16[512,4096]{1,0:T(8,128)(2,1)}, u32[]{:S(2)}) copy-start(bf16[512,4096]{1,0:T(8,128)(2,1)} %copy-done.3) | copy-start | bytes 12582916
  31.1 14.9 %copy-start.6 = (s32[64,64]{1,0:T(8,128)S(1)}, s32[64,64]{1,0:T(8,128)}, u32[]{:S(2)}) copy-start(s32[64,64]{1,0:T(8,128)} %param.13) | copy-start | bytes 49156
  41.3 64.0 %all-gather.7.cloned.1.call-start = ((), (), s32[]{:S(2)}) async-start(), calls=%async_computation.6 | async-start | bytes 3962880 | tf_op jit(solution)/shard_map/all_gather | solution.py:204
  42.3 13.8 %all-to-all-start.1 = ((bf16[4,512,128]{2,1,0:T(8,128)(2,1)}), bf16[4,512,128]{2,1,0:T(8,128)(2,1)S(1)}, u32[]{:S(2)}, u32[]{:S(2)}) async-start(bf16[4,512,128]{2,1,0:T(8,128)(2,1)} %fusion.21), calls=%async_computation.1 | async-start | bytes 1048576 | tf_op jit(solution)/shard_map/all_to_all | solution.py:189
  56.1 0.8 copy-start.5
  162.9 31.1 %all-to-all-start.3 = ((bf16[8,64,2048]{2,1,0:T(8,128)(2,1)}), bf16[8,64,2048]{2,1,0:T(8,128)(2,1)S(1)}, u32[]{:S(2)}, u32[]{:S(2)}) async-start(bf16[8,64,2048]{2,1,0:T(8,128)(2,1)} %bitcast.56), calls=%async_computation.3 | async-start | bytes 4194304 | tf_op jit(solution)/shard_map/all_to_all | solution.py:222
  194.0 33.1 %copy-start.1 = (f32[16,4096]{1,0:T(8,128)S(1)}, f32[16,4096]{1,0:T(8,128)}, u32[]{:S(2)}) copy-start(f32[16,4096]{1,0:T(8,128)} %param.10) | copy-start | bytes 786436
  194.0 30.3 %all-to-all-start.4 = ((bf16[8,64,2048]{2,1,0:T(8,128)(2,1)}), bf16[8,64,2048]{2,1,0:T(8,128)(2,1)}, u32[]{:S(2)}, u32[]{:S(2)}) async-start(bf16[8,64,2048]{2,1,0:T(8,128)(2,1)} %bitcast.55), calls=%async_computation.4 | async-start | bytes 4194304 | tf_op jit(solution)/shard_map/all_to_all | solution.py:222
Sparse Core Ops, SparseCore 0:
  41.4 22.6 all-gather.4
  65.7 39.5 all-gather.6

commit v7 on v5

--- a/solution.py
+++ b/solution.py
@@ -168,9 +168,10 @@
     level_hot = (level_rows[:, None] == level_ids).astype(jnp.float32)
     modulation = jnp.dot(level_hot, mod_table, precision=lax.Precision.HIGHEST)
     moduled = (activations.astype(jnp.float32) * (1.0 + modulation)).astype(jnp.bfloat16)
-    kv_proj = jnp.einsum(
-        "td,dchk->hctk", moduled, qkv_weight[:, 1:3], preferred_element_type=jnp.float32
-    ).astype(jnp.bfloat16)
+    k_proj, v_proj = [
+        jnp.einsum("td,dhk->htk", moduled, qkv_weight[:, c], preferred_element_type=jnp.float32).astype(jnp.bfloat16)
+        for c in (1, 2)
+    ]
     lane = head_size
     clip_rows = tok // lane
     pad_rows = -clip_rows % 8
@@ -178,7 +179,7 @@
         [clip_of.astype(jnp.bfloat16).reshape(clip_rows, lane), jnp.zeros((pad_rows, lane), jnp.bfloat16)]
     )
     kv_part = jnp.concatenate(
-        [kv_proj.reshape(heads_here, 2 * tok, lane), jnp.broadcast_to(clip_slab, (heads_here,) + clip_slab.shape)],
+        [k_proj, v_proj, jnp.broadcast_to(clip_slab, (heads_here,) + clip_slab.shape)],
         axis=1,
     )
     exch = lax.all_to_all(kv_part, "yc", 0, 0, tiled=True)

time: 229 us -> 235 us (1.026)
  matrix products: 18 us -> 21.7 us
  local copies, waits for them, and re-layouts: 9.37 us -> 12.7 us
    slice x4 -> x1, local copies, waits for them, and re-layouts: 2.19 us -> 9.03 us  [per_device_body(): qkv_weight[:, c]]
    dot_general x1, matrix products: 3.16 us -> 6.6 us  [per_device_body(): jnp.einsum('td,dhk->htk', moduled, qkv_weight[:, 0], preferred_element_ty...]
    unnamed x15, local copies, waits for them, and re-layouts: 4.25 us -> 0.82 us
    dot_general x1 -> x2, matrix products: 4.49 us -> 4.76 us  [per_device_body(): jnp.einsum('td,dhk->htk', moduled, qkv_weight[:, c], preferred_element_ty...]
  transfers between devices with their start and end apart: 4 -> 4, of which waited for: 3 -> 3; matrix products, arithmetic and copies ran while one was open for 4% -> 5% of each run, Pallas kernels for 5% -> 5%
where the time goes in v7:
time: 235 us; the launch traced here: 232 us
  blocking collectives  68.2 us (29%)
  waiting for transfers between devices  51.4 us (22%)
  Pallas kernels  47.4 us (20%)
  matrix products  21.7 us (9%)
  between operations  13.5 us (6%)
  local copies, waits for them, and re-layouts  12.7 us (5%)
  other arithmetic  9.19 us (4%)
  starting transfers between devices  8.17 us (3%)
    all_to_all x1, blocking collectives, per_device_body(): parts = lax.all_to_all(parts, 'head', 0, 0)  53.4 us
    pallas_call x2, Pallas kernels, attend_remote(): pl.pallas_call(kernel, grid_spec=grid_spec, out_shape=out_shape, compiler...  35.8 us
    all_gather x2, waiting for transfers between devices, per_device_body(): gathered.append(lax.all_gather(exch[lo:hi], 'x', axis=0))  35.3 us
    all_to_all x1, blocking collectives, per_device_body(): lax.all_to_all(attended.reshape(heads_here, tok, lane), 'yc', 0, 0, tiled...  14.7 us
    pallas_call x1, Pallas kernels, attend_local(): pl.pallas_call(functools.partial(local_kernel, scale=scale), grid=(nsteps...  11.6 us
    all_to_all x1, waiting for transfers between devices, per_device_body(): exch = lax.all_to_all(kv_part, 'yc', 0, 0, tiled=True)  9.42 us
    slice x1, local copies, waits for them, and re-layouts, per_device_body(): qkv_weight[:, c]  9.03 us
    all_to_all x1, waiting for transfers between devices, per_device_body(): exch_q = lax.all_to_all(q_part, 'yc', 0, 0, tiled=True)  6.66 us
  transfers between devices with their start and end apart: 4, of which 3 were waited for; matrix products, arithmetic and copies ran while one was open for 5% of the time, Pallas kernels for 5%

profile of v7, /device:TPU:6, one launch (start us, length us, event | category | flops | bytes accessed | tf_op | source)
XLA Modules:
  0.0 232.3 jit_solution(18201273660357820827)
XLA Ops:
  6.5 9.0 %fusion.17 = (bf16[4096,1,4,128]{3,2,1,0:T(4,128)(2,1)S(1)}, bf16[4096,1,4,128]{3,2,1,0:T(4,128)(2,1)}, bf16[4096,1,4,128]{3,2,1,0:T(4,128)(2,1)S(1)}) fusion(bf16[4096,3,4,128]{3,2,1,0:T(4,128)(2,1)} %param.8), kind=kLoop, calls=%fused_computation.35 | loop fusion | bytes 25165824 | tf_op jit(solution)/shard_map/slice | solution.py:172
  15.7 4.1 %fusion = bf16[512,4096,1]{1,0,2:T(8,128)(2,1)S(1)} fusion(f32[16,4096]{1,0:T(8,128)S(1)} %copy-done, bf16[512,4096]{1,0:T(8,128)(2,1)S(1)} %copy-done.1, s32[512]{0:T(512)S(1)} %select_reduce_fusion), kind=kOutput, calls=%fused_computation.2 | convolution fusion | flops 411049984 | bytes 8652800 | tf_op jit(solution)/shard_map/dot_general | solution.py:169
  19.8 2.3 %fusion.8 = bf16[4,512,128]{2,1,0:T(8,128)(2,1)S(1)} fusion(bf16[512,4096,1]{1,0,2:T(8,128)(2,1)S(1)} %fusion, bf16[4096,1,4,128]{3,2,1,0:T(4,128)(2,1)S(1)} %get-tuple-element.23), kind=kOutput, calls=%fused_computation.15 | convolution fusion | flops 2147745792 | bytes 8912896 | tf_op jit(solution)/shard_map/td,dhk->htk/dot_general | solution.py:172
  22.2 2.4 %fusion.9 = bf16[4,512,128]{2,1,0:T(8,128)(2,1)S(1)} fusion(bf16[512,4096,1]{1,0,2:T(8,128)(2,1)S(1)} %fusion, bf16[4096,1,4,128]{3,2,1,0:T(4,128)(2,1)S(1)} %get-tuple-element.21), kind=kOutput, calls=%fused_computation.16 | convolution fusion | flops 2147745792 | bytes 8912896 | tf_op jit(solution)/shard_map/td,dhk->htk/dot_general | solution.py:172
  24.6 1.1 pad_maximum_fusion
  25.8 4.5 %all-to-all-start = ((bf16[4,1032,128]{2,1,0:T(8,128)(2,1)}), bf16[4,1032,128]{2,1,0:T(8,128)(2,1)S(1)}, u32[]{:S(2)}, u32[]{:S(2)}) async-start(bf16[4,1032,128]{2,1,0:T(8,128)(2,1)} %pad_maximum_fusion), calls=%async_computation | async-start | bytes 2113536 | tf_op jit(solution)/shard_map/all_to_all | solution.py:185
  30.2 6.6 %fusion.10 = bf16[4,512,128]{2,1,0:T(8,128)(2,1)} fusion(bf16[512,4096,1]{1,0,2:T(8,128)(2,1)} %copy-done.2, bf16[4096,1,4,128]{3,2,1,0:T(4,128)(2,1)} %get-tuple-element.22), kind=kOutput, calls=%fused_computation.17 | convolution fusion | flops 2147745792 | bytes 8912896 | tf_op jit(solution)/shard_map/td,dhk->htk/dot_general | solution.py:186
  36.8 9.4 %all-to-all-done = bf16[4,1032,128]{2,1,0:T(8,128)(2,1)S(1)} async-done(((bf16[4,1032,128]{2,1,0:T(8,128)(2,1)}), bf16[4,1032,128]{2,1,0:T(8,128)(2,1)S(1)}, u32[]{:S(2)}, u32[]{:S(2)}) %all-to-all-start) | async-done | bytes 1056800 | tf_op jit(solution)/shard_map/all_to_all | solution.py:185
  47.1 1.0 slice.36
  48.1 3.7 %all-to-all-start.1 = ((bf16[4,512,128]{2,1,0:T(8,128)(2,1)}), bf16[4,512,128]{2,1,0:T(8,128)(2,1)S(1)}, u32[]{:S(2)}, u32[]{:S(2)}) async-start(bf16[4,512,128]{2,1,0:T(8,128)(2,1)} %fusion.10), calls=%async_computation.1 | async-start | bytes 1048576 | tf_op jit(solution)/shard_map/all_to_all | solution.py:190
  51.8 1.5 convolution_convert_fusion.qvis_ref
  53.3 1.1 fusion.18
  54.4 0.8 fusion.14.kh_ref
  55.2 6.7 %all-to-all-done.1 = bf16[4,512,128]{2,1,0:T(8,128)(2,1)S(1)} async-done(((bf16[4,512,128]{2,1,0:T(8,128)(2,1)}), bf16[4,512,128]{2,1,0:T(8,128)(2,1)S(1)}, u32[]{:S(2)}, u32[]{:S(2)}) %all-to-all-start.1) | async-done | bytes 524320 | tf_op jit(solution)/shard_map/all_to_all | solution.py:190
  61.9 0.8 copy-done.3
  62.6 11.6 %shard_map.73 = (f32[2048,128]{1,0:T(8,128)}, f32[2048,128]{1,0:T(8,128)}, f32[2048,128]{1,0:T(8,128)}) custom-call(bf16[2048,64]{1,0:T(8,128)(2,1)} %convolution_convert_fusion.qvis_ref, bf16[2048,128]{1,0:T(8,128)(2,1)} %bitcast.58, bf16[2048,128]{1,0:T(8,128)(2,1)} %bitcast.63, bf16[2048,128]{1,0:T(8,128)(2,1)} %bitcast.62, bf16[64,2048]{1,0:T(8,128)(2,1)} %fusion.14.kh_ref), custom_call_target="tpu_custom_call" | custom-call | flops 2684354560 | bytes 4194304 | tf_op jit(solution)/shard_map/pallas_call | solution.py:77
  75.7 35.3 %all-gather.7.cloned.1.call-done = bf16[12,1032,128]{2,1,0:T(8,128)(2,1)} async-done(((bf16[3,1032,128]{2,1,0:T(8,128)(2,1)}), bf16[12,1032,128]{2,1,0:T(8,128)(2,1)}) %all-gather.7.cloned.1.call-update) | async-done | bytes 3170320 | tf_op jit(solution)/shard_map/all_gather | solution.py:205
  111.8 1.1 fusion.4.kh_ref
  112.9 25.1 %shard_map.74 = (f32[2048,128]{1,0:T(8,128)}, f32[2048,128]{1,0:T(8,128)}, f32[2048,128]{1,0:T(8,128)}) custom-call(s32[1]{0:T(128)} %bitcast.own_ref, bf16[2048,64]{1,0:T(8,128)(2,1)} %convolution_convert_fusion.qvis_ref, bf16[2048,128]{1,0:T(8,128)(2,1)} %bitcast.59, bf16[4,3,1032,128]{3,2,1,0:T(8,128)(2,1)} %bitcast.67, ...), custom_call_target="tpu_custom_call" | custom-call | flops 6039797760 | bytes 5505024 | tf_op jit(solution)/shard_map/pallas_call | solution.py:145
  138.0 10.6 %shard_map.75 = bf16[2048,128]{1,0:T(8,128)(2,1)} custom-call(s32[1]{0:T(128)} %bitcast.own_ref, bf16[2048,64]{1,0:T(8,128)(2,1)} %convolution_convert_fusion.qvis_ref, bf16[2048,128]{1,0:T(8,128)(2,1)} %bitcast.60, bf16[4,1,1032,128]{3,2,1,0:T(8,128)(2,1)} %bitcast.70, bf16[4,1,1032,128]{3,2,1,0:T(8,128)(2,1)} %bitcast.71, ...), custom_call_target="tpu_custom_call" | custom-call | flops 2013265920 | bytes 3932160 | tf_op jit(solution)/shard_map/pallas_call | solution.py:145
  148.7 14.7 %all_to_all.20 = bf16[4,512,128]{2,1,0:T(8,128)(2,1)S(1)} all-to-all(bf16[4,512,128]{2,1,0:T(8,128)(2,1)} %bitcast.61), channel_id=1, replica_groups=mesh['x'=4,'yc'=4,'head'=8] {'yc'}, dimensions={0} | all-to-all | bytes 1048576 | tf_op jit(solution)/shard_map/all_to_all | solution.py:212
  163.4 4.7 %bitcast_convert_fusion = bf16[512,4096]{1,0:T(8,128)(2,1)S(1)} fusion(bf16[4,128,4096]{2,1,0:T(8,128)(2,1)} %param.9, bf16[4,512,128]{2,1,0:T(8,128)(2,1)S(1)} %all_to_all.20), kind=kOutput, calls=%fused_computation | convolution fusion | flops 2149580800 | bytes 8912896 | tf_op jit(solution)/shard_map/dot_general | solution.py:215
  168.2 53.4 %all_to_all.21 = bf16[8,64,4096]{2,1,0:T(8,128)(2,1)} all-to-all(bf16[8,64,4096]{2,1,0:T(8,128)(2,1)S(1)} %bitcast.57), channel_id=1, replica_groups=mesh['x'=4,'yc'=4,'head'=8] {'head'}, dimensions={0} | all-to-all | bytes 8388608 | tf_op jit(solution)/shard_map/all_to_all | solution.py:218
  221.6 3.8 %reduce_sum.22 = bf16[64,4096]{1,0:T(8,128)(2,1)} reduce(bf16[8,64,4096]{2,1,0:T(8,128)(2,1)} %all_to_all.21, bf16[]{:T(256)} %constant.13.clone.1), dimensions={0}, to_apply=%region_1.2 | reduce | flops 1835008 | bytes 4718594 | tf_op jit(solution)/shard_map/reduce_sum | solution.py:219
  (30 shorter events, 3.2 us)
Async XLA Ops:
  6.5 9.2 %copy-start = (f32[16,4096]{1,0:T(8,128)S(1)}, f32[16,4096]{1,0:T(8,128)}, u32[]{:S(2)}) copy-start(f32[16,4096]{1,0:T(8,128)} %param.10) | copy-start | bytes 786436
  6.5 9.0 %copy-start.5 = (s32[512]{0:T(512)S(1)}, s32[512]{0:T(512)}, u32[]{:S(2)}) copy-start(s32[512]{0:T(512)} %param.12) | copy-start | bytes 6148
  6.5 9.0 %copy-start.6 = (s32[64]{0:T(128)S(1)}, s32[64]{0:T(128)}, u32[]{:S(2)}) copy-start(s32[64]{0:T(128)} %param.11) | copy-start | bytes 772
  6.5 9.2 %copy-start.1 = (bf16[512,4096]{1,0:T(8,128)(2,1)S(1)}, bf16[512,4096]{1,0:T(8,128)(2,1)}, u32[]{:S(2)}) copy-start(bf16[512,4096]{1,0:T(8,128)(2,1)} %param.7) | copy-start | bytes 12582916
  19.8 2.3 %copy-start.2 = (bf16[512,4096,1]{1,0,2:T(8,128)(2,1)}, bf16[512,4096,1]{1,0,2:T(8,128)(2,1)S(1)}, u32[]{:S(2)}) copy-start(bf16[512,4096,1]{1,0,2:T(8,128)(2,1)S(1)} %fusion) | copy-start | bytes 12582916
  25.8 20.5 %all-to-all-start = ((bf16[4,1032,128]{2,1,0:T(8,128)(2,1)}), bf16[4,1032,128]{2,1,0:T(8,128)(2,1)S(1)}, u32[]{:S(2)}, u32[]{:S(2)}) async-start(bf16[4,1032,128]{2,1,0:T(8,128)(2,1)} %pad_maximum_fusion), calls=%async_computation | async-start | bytes 2113536 | tf_op jit(solution)/shard_map/all_to_all | solution.py:185
  30.2 44.0 %all-gather.5.cloned.1.call-start = ((), (), s32[]{:S(2)}) async-start(), calls=%async_computation.4 | async-start | bytes 1320960 | tf_op jit(solution)/shard_map/all_gather | solution.py:205
  36.8 14.9 %copy-start.4 = (s32[64,64]{1,0:T(8,128)S(1)}, s32[64,64]{1,0:T(8,128)}, u32[]{:S(2)}) copy-start(s32[64,64]{1,0:T(8,128)} %param.13) | copy-start | bytes 49156
  47.0 64.0 %all-gather.7.cloned.1.call-start = ((), (), s32[]{:S(2)}) async-start(), calls=%async_computation.5 | async-start | bytes 3962880 | tf_op jit(solution)/shard_map/all_gather | solution.py:205
  48.1 13.8 %all-to-all-start.1 = ((bf16[4,512,128]{2,1,0:T(8,128)(2,1)}), bf16[4,512,128]{2,1,0:T(8,128)(2,1)S(1)}, u32[]{:S(2)}, u32[]{:S(2)}) async-start(bf16[4,512,128]{2,1,0:T(8,128)(2,1)} %fusion.10), calls=%async_computation.1 | async-start | bytes 1048576 | tf_op jit(solution)/shard_map/all_to_all | solution.py:190
  61.9 0.8 copy-start.3
Sparse Core Ops, SparseCore 0:
  47.1 22.6 all-gather.4
  71.5 39.4 all-gather.6
